TPU v7x, 256 devices: a whole 4x4x8 slice. The times are simulated.
256 devices in a mesh: dp: 8 (over z_lo, x), expert: 32 (over z_hi, y, core).
Axes of the slice: x: 4, y: 4, z: 8 (z_hi: 4, z_lo: 2; z = z_hi * 2 + z_lo), core: 2. Of those that a mesh axis runs over, the one named last changes fastest.
Arguments:
- tokens: bfloat16 [8192, 4096], P('expert', 'dp'), may hold values from -6 to 6
- out_grad: bfloat16 [8192, 4096], P('expert', 'dp'), may hold values from -3 to 3
- expert_ids: int32 [8192, 2], P('expert'), may hold values from 0 to 31, as said below
- gate_probs: float32 [8192, 2], P('expert'), may hold values from 0.25 to 1
- w_gate: bfloat16 [32, 4096, 1024], P('expert', 'dp'), may hold values from -0.09375 to 0.09375
- w_up: bfloat16 [32, 4096, 1024], P('expert', 'dp'), may hold values from -0.09375 to 0.09375
- w_down: bfloat16 [32, 1024, 4096], P('expert', None, 'dp'), may hold values from -0.1875 to 0.1875
Outputs:
- token_grad: bfloat16 [8192, 4096], P('expert', 'dp')
- grad_w_gate: float32 [32, 4096, 1024], P('expert', 'dp')
- grad_w_up: float32 [32, 4096, 1024], P('expert', 'dp')
- grad_w_down: float32 [32, 1024, 4096], P('expert', None, 'dp')
Inputs may be any that keep to these rules, and one draw needn't show every extreme that they name: `expert_ids`: A token's two ids differ. Among the tokens of one aligned block of 256 tokens no expert is named more than 32 times; 4 experts, the same for every block, are named exactly 32 times in each block.
All inputs are finite; a program needn't handle non-finite values.
Results may differ from a plain program's by a relative error of at most 0.02.
Values may be sent and summed in bfloat16 or wider, within the bound.
No kernel may reach another device: no remote copies, remote signals or barrier semaphores. Data moves between devices by JAX's collectives and lax.ppermute only.
A program may use at most 64 MiB of HBM per device.

v0:
```python
import jax
import jax.numpy as jnp
from jax import lax
from jax.sharding import PartitionSpec as P

MOST = 32


contract_rows = (((0,), (0,)), ((), ()))
contract_cols = (((1,), (1,)), ((), ()))


def silu_parts(pre_gate):
    sigmoid_gate = jax.nn.sigmoid(pre_gate)
    return (pre_gate * sigmoid_gate, sigmoid_gate * (1.0 + pre_gate * (1.0 - sigmoid_gate)))


def local_grads(pre_gate, pre_up, grad_act):
    active, slope_gate = silu_parts(pre_gate)
    hidden = (active * pre_up).astype(jnp.bfloat16)
    grad_gate = (grad_act * pre_up * slope_gate).astype(jnp.bfloat16)
    grad_up = (grad_act * active).astype(jnp.bfloat16)
    return (hidden, grad_gate, grad_up)


def shards(tokens, out_grad, expert_ids, gate_probs, w_gate, w_up, w_down):
    tok_rows, slab_width = tokens.shape
    owners = lax.axis_size("expert")
    experts = owners * w_gate.shape[0]
    pick_ids = expert_ids.T.reshape(-1)
    onehot = (pick_ids[:, None] == jnp.arange(experts, dtype=jnp.int32)[None, :]).astype(jnp.int32)
    rank_in = jnp.sum((jnp.cumsum(onehot, axis=0) - 1) * onehot, axis=1)
    slot_of = pick_ids * MOST + rank_in
    placing = (jnp.arange(experts * MOST, dtype=jnp.int32)[:, None] == slot_of[None, :]).astype(
        jnp.bfloat16
    )
    row_pick = jnp.concatenate([tokens, tokens], axis=0)
    grad_pick = jnp.concatenate([out_grad, out_grad], axis=0)
    scaled = (gate_probs.T.reshape(-1)[:, None] * grad_pick.astype(jnp.float32)).astype(
        jnp.bfloat16
    )
    send_tokens = (
        jnp.dot(placing, row_pick, preferred_element_type=jnp.float32)
        .astype(jnp.bfloat16)
        .reshape(experts, MOST, slab_width)
    )
    send_grads = (
        jnp.dot(placing, scaled, preferred_element_type=jnp.float32)
        .astype(jnp.bfloat16)
        .reshape(experts, MOST, slab_width)
    )
    arrived_tokens, arrived_grads = (
        lax.all_to_all(send_tokens, "expert", split_axis=0, concat_axis=0, tiled=True),
        lax.all_to_all(send_grads, "expert", split_axis=0, concat_axis=0, tiled=True),
    )
    flat_tokens = arrived_tokens.reshape(-1, slab_width)
    flat_grads = arrived_grads.reshape(-1, slab_width)
    gate_mat = w_gate[0]
    up_mat = w_up[0]
    down_mat = w_down[0]
    part_gate = jnp.dot(flat_tokens, gate_mat, preferred_element_type=jnp.float32)
    part_up = jnp.dot(flat_tokens, up_mat, preferred_element_type=jnp.float32)
    part_act = lax.dot_general(
        flat_grads, down_mat, contract_cols, preferred_element_type=jnp.float32
    )
    pre_gate, pre_up, grad_act = (
        lax.psum(part_gate.astype(jnp.bfloat16), "dp").astype(jnp.float32),
        lax.psum(part_up.astype(jnp.bfloat16), "dp").astype(jnp.float32),
        lax.psum(part_act.astype(jnp.bfloat16), "dp").astype(jnp.float32),
    )
    hidden, grad_gate, grad_up = local_grads(pre_gate, pre_up, grad_act)
    slot_grad = lax.dot_general(
        grad_gate, gate_mat, contract_cols, preferred_element_type=jnp.float32
    )
    slot_grad = slot_grad + lax.dot_general(
        grad_up, up_mat, contract_cols, preferred_element_type=jnp.float32
    )
    gate_grads = lax.dot_general(
        flat_tokens, grad_gate, contract_rows, preferred_element_type=jnp.float32
    )[None]
    up_grads = lax.dot_general(
        flat_tokens, grad_up, contract_rows, preferred_element_type=jnp.float32
    )[None]
    down_grads = lax.dot_general(
        hidden, flat_grads, contract_rows, preferred_element_type=jnp.float32
    )[None]
    returned = lax.all_to_all(
        slot_grad.reshape(experts, MOST, slab_width).astype(jnp.bfloat16),
        "expert",
        split_axis=0,
        concat_axis=0,
        tiled=True,
    ).astype(jnp.float32)
    flat_back = returned.reshape(experts * MOST, slab_width)
    per_pick = jnp.take(flat_back, slot_of, axis=0)
    token_grad = (per_pick[:tok_rows] + per_pick[tok_rows:]).astype(jnp.bfloat16)
    return (token_grad, gate_grads, up_grads, down_grads)


def solution(mesh):
    in_specs = (
        P("expert", "dp"),
        P("expert", "dp"),
        P("expert", None),
        P("expert", None),
        P("expert", "dp", None),
        P("expert", "dp", None),
        P("expert", None, "dp"),
    )
    out_specs = (
        P("expert", "dp"),
        P("expert", "dp", None),
        P("expert", "dp", None),
        P("expert", None, "dp"),
    )
    return jax.shard_map(shards, mesh=mesh, in_specs=in_specs, out_specs=out_specs, check_vma=False)
```

profile of v0, /device:TPU:32, one launch (start us, length us, event | category | flops | bytes accessed | tf_op | source)
XLA Modules:
  0.0 298.3 jit_solution(11739349572453561312)
XLA Ops:
  7.2 0.0 copy-start
  7.2 0.8 eq.39
  8.0 1.2 reduce-window.6
  9.1 0.2 slice_reduce_fusion
  9.4 0.7 copy.13
  10.1 0.1 fusion.35
  10.2 2.8 fusion.17
  13.0 10.6 %all-to-all-start.1 = ((bf16[32,32,512]{2,1,0:T(8,128)(2,1)}), bf16[32,32,512]{2,1,0:T(8,128)(2,1)S(1)}, u32[]{:S(2)}, u32[]{:S(2)}) async-start(bf16[32,32,512]{2,1,0:T(8,128)(2,1)} %bitcast.6), calls=%async_computation.1 | async-start | bytes 2097152 | tf_op jit(solution)/shard_map/all_to_all | solution.py:53
  23.6 1.8 fusion.16
  25.4 27.1 %all-to-all-done.1 = bf16[32,32,512]{2,1,0:T(8,128)(2,1)S(1)} async-done(((bf16[32,32,512]{2,1,0:T(8,128)(2,1)}), bf16[32,32,512]{2,1,0:T(8,128)(2,1)S(1)}, u32[]{:S(2)}, u32[]{:S(2)}) %all-to-all-start.1) | async-done | bytes 1048608 | tf_op jit(solution)/shard_map/all_to_all | solution.py:53
  52.5 4.6 %all-to-all-start = ((bf16[32,32,512]{2,1,0:T(8,128)(2,1)}), bf16[32,32,512]{2,1,0:T(8,128)(2,1)S(1)}, u32[]{:S(2)}, u32[]{:S(2)}) async-start(bf16[32,32,512]{2,1,0:T(8,128)(2,1)} %bitcast.73), calls=%async_computation | async-start | bytes 2097152 | tf_op jit(solution)/shard_map/all_to_all | solution.py:54
  57.1 0.0 all-reduce.3.cloned.1.call-start
  57.2 0.0 copy-start.8
  57.2 2.6 convolution_convert_fusion
  59.7 2.6 convolution_convert_fusion.1
  62.3 18.0 %all-to-all-done = bf16[32,32,512]{2,1,0:T(8,128)(2,1)S(1)} async-done(((bf16[32,32,512]{2,1,0:T(8,128)(2,1)}), bf16[32,32,512]{2,1,0:T(8,128)(2,1)S(1)}, u32[]{:S(2)}, u32[]{:S(2)}) %all-to-all-start) | async-done | bytes 1048608 | tf_op jit(solution)/shard_map/all_to_all | solution.py:54
  80.4 3.8 %convolution_convert_fusion.2 = bf16[1024,1024]{1,0:T(8,128)(2,1)} fusion(bf16[1024,512]{1,0:T(8,128)(2,1)S(1)} %bitcast.70, bf16[1,1024,512]{2,1,0:T(8,128)(2,1)} %param.13), kind=kOutput, calls=%fused_computation.23 | convolution fusion | flops 1074790400 | bytes 4194304 | tf_op jit(solution)/shard_map/dot_general | solution.py:63
  84.2 0.0 all-reduce.3.cloned.1.call-update
  84.2 152.7 %all-reduce.3.cloned.1.call-done = (bf16[1024,1024]{1,0:T(8,128)(2,1)}, bf16[1024,1024]{1,0:T(8,128)(2,1)}, bf16[1024,1024]{1,0:T(8,128)(2,1)}) async-done(((bf16[1024,1024]{1,0:T(8,128)(2,1)}, bf16[1024,1024]{1,0:T(8,128)(2,1)}, bf16[1024,1024]{1,0:T(8,128)(2,1)}), (bf16[1024,1024]{1,0:T(8,128)(2,1)}, bf16[1024,1024]{1,0:T(8,128)(2,1)}, bf16[1024,1024]{1,0:T(8,128)(2,1)})) %all-reduce.3.cloned.1.call-update) | async-done | bytes 6291472 | tf_op jit(solution)/shard_map/psum | solution.py:68
  236.9 4.2 %fusion = (bf16[1024,1024]{1,0:T(8,128)(2,1)S(1)}, bf16[1024,1024]{1,0:T(8,128)(2,1)S(1)}) fusion(bf16[1024,1024]{1,0:T(8,128)(2,1)} %get-tuple-element.5, bf16[1024,1024]{1,0:T(8,128)(2,1)} %get-tuple-element.6, bf16[1024,1024]{1,0:T(8,128)(2,1)} %get-tuple-element.4), kind=kLoop, calls=%fused_computation.7 | loop fusion | flops 16777216 | bytes 10485760 | tf_op jit(solution)/shard_map/convert_element_type | solution.py:22
  241.2 1.3 fusion.18
  242.5 0.7 copy-done.9
  243.2 2.3 add_convert_fusion
  245.5 10.3 %all-to-all-start.2 = ((bf16[32,32,512]{2,1,0:T(8,128)(2,1)}), bf16[32,32,512]{2,1,0:T(8,128)(2,1)}, u32[]{:S(2)}, u32[]{:S(2)}) async-start(bf16[32,32,512]{2,1,0:T(8,128)(2,1)} %bitcast.72), calls=%async_computation.2 | async-start | bytes 2097152 | tf_op jit(solution)/shard_map/all_to_all | solution.py:87
  255.9 4.3 %convolution_bitcast_fusion = f32[1,512,1024]{2,1,0:T(8,128)} fusion(bf16[1024,512]{1,0:T(8,128)(2,1)S(1)} %bitcast.68, bf16[1024,1024]{1,0:T(8,128)(2,1)} %copy-done.3), kind=kOutput, calls=%fused_computation.25 | convolution fusion | flops 1073741824 | bytes 5242880 | tf_op jit(solution)/shard_map/dot_general | solution.py:81
  260.2 2.6 convolution_bitcast_fusion.1
  262.8 2.8 fusion.13
  265.6 19.8 %all-to-all-done.2 = bf16[32,32,512]{2,1,0:T(8,128)(2,1)} async-done(((bf16[32,32,512]{2,1,0:T(8,128)(2,1)}), bf16[32,32,512]{2,1,0:T(8,128)(2,1)}, u32[]{:S(2)}, u32[]{:S(2)}) %all-to-all-start.2) | async-done | bytes 1048608 | tf_op jit(solution)/shard_map/all_to_all | solution.py:87
  285.5 1.5 bitcast_convert_fusion
  287.0 2.3 gather_fusion
  289.3 1.4 broadcast_select_fusion
  290.7 0.8 fusion.26
  (28 shorter events, 0.1 us)
Async XLA Ops:
  7.2 50.0 %copy-start = (bf16[1,512,1024]{2,1,0:T(8,128)(2,1)S(1)}, bf16[1,512,1024]{2,1,0:T(8,128)(2,1)}, u32[]{:S(2)}) copy-start(bf16[1,512,1024]{2,1,0:T(8,128)(2,1)} %param.11) | copy-start | bytes 3145732
  10.2 13.4 %copy-start.7 = (f32[256,2]{0,1:T(2,128)S(1)}, f32[256,2]{0,1:T(2,128)}, u32[]{:S(2)}) copy-start(f32[256,2]{0,1:T(2,128)} %param.10) | copy-start | bytes 6148
  10.2 13.4 %copy-start.10 = (bf16[256,512]{1,0:T(8,128)(2,1)S(1)}, bf16[256,512]{1,0:T(8,128)(2,1)}, u32[]{:S(2)}) copy-start(bf16[256,512]{1,0:T(8,128)(2,1)} %param.8) | copy-start | bytes 786436
  13.0 39.5 %all-to-all-start.1 = ((bf16[32,32,512]{2,1,0:T(8,128)(2,1)}), bf16[32,32,512]{2,1,0:T(8,128)(2,1)S(1)}, u32[]{:S(2)}, u32[]{:S(2)}) async-start(bf16[32,32,512]{2,1,0:T(8,128)(2,1)} %bitcast.6), calls=%async_computation.1 | async-start | bytes 2097152 | tf_op jit(solution)/shard_map/all_to_all | solution.py:53
  52.5 27.9 %all-to-all-start = ((bf16[32,32,512]{2,1,0:T(8,128)(2,1)}), bf16[32,32,512]{2,1,0:T(8,128)(2,1)S(1)}, u32[]{:S(2)}, u32[]{:S(2)}) async-start(bf16[32,32,512]{2,1,0:T(8,128)(2,1)} %bitcast.73), calls=%async_computation | async-start | bytes 2097152 | tf_op jit(solution)/shard_map/all_to_all | solution.py:54
  57.1 179.8 %all-reduce.3.cloned.1.call-start = ((), (), s32[]{:S(2)}) async-start(), calls=%async_computation.3 | async-start | bytes 12582912 | tf_op jit(solution)/shard_map/psum | solution.py:68
  57.2 2.6 copy-start.8
  241.2 1.3 copy-start.1
  241.2 4.3 %copy-start.3 = (bf16[1024,1024]{1,0:T(8,128)(2,1)}, bf16[1024,1024]{1,0:T(8,128)(2,1)S(1)}, u32[]{:S(2)}) copy-start(bf16[1024,1024]{1,0:T(8,128)(2,1)S(1)} %get-tuple-element.9) | copy-start | bytes 6291460
  241.2 2.0 copy-start.9
  245.5 10.3 %copy-start.6 = (s32[256,2]{0,1:T(2,128)S(1)}, s32[256,2]{0,1:T(2,128)}, u32[]{:S(2)}) copy-start(s32[256,2]{0,1:T(2,128)} %param.9) | copy-start | bytes 6148
  245.5 40.0 %all-to-all-start.2 = ((bf16[32,32,512]{2,1,0:T(8,128)(2,1)}), bf16[32,32,512]{2,1,0:T(8,128)(2,1)}, u32[]{:S(2)}, u32[]{:S(2)}) async-start(bf16[32,32,512]{2,1,0:T(8,128)(2,1)} %bitcast.72), calls=%async_computation.2 | async-start | bytes 2097152 | tf_op jit(solution)/shard_map/all_to_all | solution.py:87
  255.9 4.3 %copy-start.2 = (bf16[1024,1024]{1,0:T(8,128)(2,1)S(1)}, bf16[1024,1024]{1,0:T(8,128)(2,1)}, u32[]{:S(2)}) copy-start(bf16[1024,1024]{1,0:T(8,128)(2,1)} %copy-done.1) | copy-start | bytes 6291460
  260.2 2.6 copy-start.4
  260.2 2.6 copy-start.5
Sparse Core Ops, SparseCore 0:
  84.4 152.4 all-reduce.2
where the time goes:
time: 299 us; the launch traced here: 298 us
  waiting for transfers between devices  218 us (73%)
  matrix products  26.8 us (9%)
  starting transfers between devices  25.6 us (9%)
  between operations  14.2 us (5%)
  other arithmetic  9.22 us (3%)
  local copies, waits for them, and re-layouts  4.81 us (2%)
    psum x1, waiting for transfers between devices, shards(): lax.psum(part_up.astype(jnp.bfloat16), 'dp').astype(jnp.float32)  153 us
    all_to_all x1, waiting for transfers between devices, shards(): lax.all_to_all(send_tokens, 'expert', split_axis=0, concat_axis=0, tiled=...  27.1 us
    all_to_all x1, waiting for transfers between devices, shards(): lax.all_to_all(slot_grad.reshape(experts, MOST, slab_width).astype(jnp.bf...  19.8 us
    all_to_all x1, waiting for transfers between devices, shards(): lax.all_to_all(send_grads, 'expert', split_axis=0, concat_axis=0, tiled=T...  18 us
    all_to_all x1, starting transfers between devices, shards(): lax.all_to_all(send_tokens, 'expert', split_axis=0, concat_axis=0, tiled=...  10.6 us
    all_to_all x1, starting transfers between devices, shards(): lax.all_to_all(slot_grad.reshape(experts, MOST, slab_width).astype(jnp.bf...  10.3 us
  transfers between devices with their start and end apart: 4, of which 4 were waited for; matrix products, arithmetic and copies ran while one was open for 6% of the time, Pallas kernels for 0%

commit v1 on v0

v1 whole, which is shorter than its diff:
```python
import jax
import jax.numpy as jnp
from jax import lax
from jax.sharding import PartitionSpec as P

MOST = 32
CHUNKS = 4


contract_rows = (((0,), (0,)), ((), ()))
contract_cols = (((1,), (1,)), ((), ()))


def silu_parts(pre_gate):
    sigmoid_gate = jax.nn.sigmoid(pre_gate)
    return (pre_gate * sigmoid_gate, sigmoid_gate * (1.0 + pre_gate * (1.0 - sigmoid_gate)))


def local_grads(pre_gate, pre_up, grad_act):
    active, slope_gate = silu_parts(pre_gate)
    hidden = (active * pre_up).astype(jnp.bfloat16)
    grad_gate = (grad_act * pre_up * slope_gate).astype(jnp.bfloat16)
    grad_up = (grad_act * active).astype(jnp.bfloat16)
    return (hidden, grad_gate, grad_up)


def shards(tokens, out_grad, expert_ids, gate_probs, w_gate, w_up, w_down):
    tok_rows, slab_width = tokens.shape
    owners = lax.axis_size("expert")
    experts = owners * w_gate.shape[0]
    hidden_width = w_gate.shape[2]
    pick_ids = expert_ids.T.reshape(-1)
    onehot = (pick_ids[:, None] == jnp.arange(experts, dtype=jnp.int32)[None, :]).astype(jnp.int32)
    rank_in = jnp.sum((jnp.cumsum(onehot, axis=0) - 1) * onehot, axis=1)
    slot_of = pick_ids * MOST + rank_in
    placing = (jnp.arange(experts * MOST, dtype=jnp.int32)[:, None] == slot_of[None, :]).astype(
        jnp.bfloat16
    )
    row_pick = jnp.concatenate([tokens, tokens], axis=0)
    grad_pick = jnp.concatenate([out_grad, out_grad], axis=0)
    scaled = (gate_probs.T.reshape(-1)[:, None] * grad_pick.astype(jnp.float32)).astype(
        jnp.bfloat16
    )
    both = jnp.concatenate([row_pick, scaled], axis=1)
    send = (
        jnp.dot(placing, both, preferred_element_type=jnp.float32)
        .astype(jnp.bfloat16)
        .reshape(experts, MOST, 2 * slab_width)
    )
    gate_mat = w_gate[0]
    up_mat = w_up[0]
    down_mat = w_down[0]
    step = MOST // CHUNKS
    gate_grads = jnp.zeros((slab_width, hidden_width), jnp.float32)
    up_grads = jnp.zeros((slab_width, hidden_width), jnp.float32)
    down_grads = jnp.zeros((hidden_width, slab_width), jnp.float32)
    received = []
    partial_list = []
    for c in range(CHUNKS):
        part = send[:, c * step : (c + 1) * step, :]
        arrived = lax.all_to_all(part, "expert", split_axis=0, concat_axis=0, tiled=True)
        flat = arrived.reshape(-1, 2 * slab_width)
        flat_tokens = flat[:, :slab_width]
        flat_grads = flat[:, slab_width:]
        part_gate = jnp.dot(flat_tokens, gate_mat, preferred_element_type=jnp.float32)
        part_up = jnp.dot(flat_tokens, up_mat, preferred_element_type=jnp.float32)
        part_act = lax.dot_general(
            flat_grads, down_mat, contract_cols, preferred_element_type=jnp.float32
        )
        partials = jnp.concatenate([part_gate, part_up, part_act], axis=1).astype(jnp.bfloat16)
        received.append((flat_tokens, flat_grads))
        partial_list.append(partials)
    back = []
    summed = None
    for c in range(CHUNKS):
        flat_tokens, flat_grads = received[c]
        partials = partial_list[c]
        if summed is not None:
            partials, _ = lax.optimization_barrier((partials, summed))
        summed = lax.psum(partials, "dp")
        wide = summed.astype(jnp.float32)
        pre_gate = wide[:, :hidden_width]
        pre_up = wide[:, hidden_width : 2 * hidden_width]
        grad_act = wide[:, 2 * hidden_width :]
        hidden, grad_gate, grad_up = local_grads(pre_gate, pre_up, grad_act)
        slot_grad = lax.dot_general(
            grad_gate, gate_mat, contract_cols, preferred_element_type=jnp.float32
        )
        slot_grad = slot_grad + lax.dot_general(
            grad_up, up_mat, contract_cols, preferred_element_type=jnp.float32
        )
        gate_grads = gate_grads + lax.dot_general(
            flat_tokens, grad_gate, contract_rows, preferred_element_type=jnp.float32
        )
        up_grads = up_grads + lax.dot_general(
            flat_tokens, grad_up, contract_rows, preferred_element_type=jnp.float32
        )
        down_grads = down_grads + lax.dot_general(
            hidden, flat_grads, contract_rows, preferred_element_type=jnp.float32
        )
        returned = lax.all_to_all(
            slot_grad.reshape(experts, step, slab_width).astype(jnp.bfloat16),
            "expert",
            split_axis=0,
            concat_axis=0,
            tiled=True,
        )
        back.append(returned)
    flat_back = jnp.concatenate(back, axis=1).astype(jnp.float32).reshape(experts * MOST, slab_width)
    per_pick = jnp.take(flat_back, slot_of, axis=0)
    token_grad = (per_pick[:tok_rows] + per_pick[tok_rows:]).astype(jnp.bfloat16)
    return (token_grad, gate_grads[None], up_grads[None], down_grads[None])


def solution(mesh):
    in_specs = (
        P("expert", "dp"),
        P("expert", "dp"),
        P("expert", None),
        P("expert", None),
        P("expert", "dp", None),
        P("expert", "dp", None),
        P("expert", None, "dp"),
    )
    out_specs = (
        P("expert", "dp"),
        P("expert", "dp", None),
        P("expert", "dp", None),
        P("expert", None, "dp"),
    )
    return jax.shard_map(shards, mesh=mesh, in_specs=in_specs, out_specs=out_specs, check_vma=False)
```

time: 299 us -> 513 us (1.72)
  waiting for transfers between devices: 218 us -> 314 us
  matrix products: 26.8 us -> 72.2 us
  blocking collectives: 0 us -> 28.1 us
  starting transfers between devices: 25.6 us -> 43.8 us
  other arithmetic: 9.22 us -> 26.9 us
    psum x1 -> x4, waiting for transfers between devices: 153 us -> 255 us  [shards(): summed = lax.psum(partials, 'dp')]
    all_to_all x0 -> x1, blocking collectives: none -> 28.1 us  [shards(): lax.all_to_all(part, 'expert', split_axis=0, concat_axis=0, tiled=True)]
    all_to_all x3 -> x7, starting transfers between devices: 25.5 us -> 43.5 us  [the longest x4 29 us: shards(): lax.all_to_all(slot_grad.reshape(experts, step, slab_width).astype(jnp.bf...]
    convert_element_type x0 -> x6, other arithmetic: none -> 10.3 us  [the longest x4 8.69 us: shards(): wide = summed.astype(jnp.float32)]
    dot_general x1 -> x4, matrix products: 2.83 us -> 12.8 us  [shards(): lax.dot_general(hidden, flat_grads, contract_rows, preferred_element_type...]
    dot_general x1 -> x4, matrix products: 2.59 us -> 11.7 us  [shards(): lax.dot_general(flat_tokens, grad_gate, contract_rows, preferred_element_...]
    concatenate x0 -> x5, other arithmetic: none -> 8.63 us  [the longest x4 7.4 us: shards(): jnp.concatenate([part_gate, part_up, part_act], axis=1).astype(jnp.bfloat16)]
    dot_general x1 -> x4, matrix products: 4.33 us -> 12.9 us  [shards(): lax.dot_general(flat_tokens, grad_up, contract_rows, preferred_element_ty...]
  transfers between devices with their start and end apart: 4 -> 11, of which waited for: 4 -> 10; matrix products, arithmetic and copies ran while one was open for 6% -> 18% of each run, Pallas kernels for 0% -> 0%
where the time goes in v1:
time: 513 us; the launch traced here: 509 us
  waiting for transfers between devices  314 us (61%)
  matrix products  72.2 us (14%)
  starting transfers between devices  43.8 us (9%)
  blocking collectives  28.1 us (5%)
  other arithmetic  26.9 us (5%)
  between operations  14.2 us (3%)
  local copies, waits for them, and re-layouts  9.01 us (2%)
    psum x4, waiting for transfers between devices, shards(): summed = lax.psum(partials, 'dp')  255 us
    all_to_all x3, waiting for transfers between devices, shards(): lax.all_to_all(part, 'expert', split_axis=0, concat_axis=0, tiled=True)  38.4 us
    all_to_all x4, starting transfers between devices, shards(): lax.all_to_all(slot_grad.reshape(experts, step, slab_width).astype(jnp.bf...  29 us
    all_to_all x1, blocking collectives, shards(): lax.all_to_all(part, 'expert', split_axis=0, concat_axis=0, tiled=True)  28.1 us
    all_to_all x4, waiting for transfers between devices, shards(): lax.all_to_all(slot_grad.reshape(experts, step, slab_width).astype(jnp.bf...  20.7 us
    all_to_all x3, starting transfers between devices, shards(): lax.all_to_all(part, 'expert', split_axis=0, concat_axis=0, tiled=True)  14.5 us
    dot_general x4, matrix products, shards(): lax.dot_general(flat_tokens, grad_up, contract_rows, preferred_element_ty...  12.9 us
    dot_general x4, matrix products, shards(): lax.dot_general(hidden, flat_grads, contract_rows, preferred_element_type...  12.8 us
  transfers between devices with their start and end apart: 11, of which 10 were waited for; matrix products, arithmetic and copies ran while one was open for 18% of the time, Pallas kernels for 0%

profile of v1, /device:TPU:32, one launch (start us, length us, event | category | flops | bytes accessed | tf_op | source)
XLA Modules:
  0.0 508.6 jit_solution(13545146943065124454)
XLA Ops:
  15.6 28.1 %all_to_all.40 = bf16[32,8,1024]{2,1,0:T(8,128)(2,1)} all-to-all(bf16[32,8,1024]{2,1,0:T(8,128)(2,1)S(1)} %get-tuple-element.20), channel_id=1, replica_groups=mesh['dp'=8,'expert'=32] {'expert'}, dimensions={0} | all-to-all | bytes 1048576 | tf_op jit(solution)/shard_map/all_to_all | solution.py:61
  43.7 5.3 %all-to-all-start.2 = ((bf16[32,8,1024]{2,1,0:T(8,128)(2,1)}), bf16[32,8,1024]{2,1,0:T(8,128)(2,1)}, u32[]{:S(2)}, u32[]{:S(2)}) async-start(bf16[32,8,1024]{2,1,0:T(8,128)(2,1)} %get-tuple-element.23), calls=%async_computation.2 | async-start | bytes 1048576 | tf_op jit(solution)/shard_map/all_to_all | solution.py:61
  53.6 13.7 %all-to-all-done.2 = bf16[32,8,1024]{2,1,0:T(8,128)(2,1)} async-done(((bf16[32,8,1024]{2,1,0:T(8,128)(2,1)}), bf16[32,8,1024]{2,1,0:T(8,128)(2,1)}, u32[]{:S(2)}, u32[]{:S(2)}) %all-to-all-start.2) | async-done | bytes 524320 | tf_op jit(solution)/shard_map/all_to_all | solution.py:61
  67.3 4.6 all-to-all-start.4
  79.2 11.0 %all-to-all-done.4 = bf16[32,8,1024]{2,1,0:T(8,128)(2,1)} async-done(((bf16[32,8,1024]{2,1,0:T(8,128)(2,1)}), bf16[32,8,1024]{2,1,0:T(8,128)(2,1)}, u32[]{:S(2)}, u32[]{:S(2)}) %all-to-all-start.4) | async-done | bytes 524320 | tf_op jit(solution)/shard_map/all_to_all | solution.py:61
  90.2 4.6 all-to-all-start.6
  103.6 13.7 %all-to-all-done.6 = bf16[32,8,1024]{2,1,0:T(8,128)(2,1)} async-done(((bf16[32,8,1024]{2,1,0:T(8,128)(2,1)}), bf16[32,8,1024]{2,1,0:T(8,128)(2,1)}, u32[]{:S(2)}, u32[]{:S(2)}) %all-to-all-start.6) | async-done | bytes 524320 | tf_op jit(solution)/shard_map/all_to_all | solution.py:61
  127.8 2.6 pad_maximum_fusion.3
  130.4 38.5 %all-reduce.5.cloned.1.call-done = bf16[256,3072]{1,0:T(8,128)(2,1)} async-done(((bf16[256,3072]{1,0:T(8,128)(2,1)}), bf16[256,3072]{1,0:T(8,128)(2,1)}) %all-reduce.5.cloned.1.call-update) | async-done | bytes 1572880 | tf_op jit(solution)/shard_map/psum | solution.py:80
  174.3 9.8 %all-to-all-start.1 = ((bf16[32,8,512]{2,1,0:T(8,128)(2,1)}), bf16[32,8,512]{2,1,0:T(8,128)(2,1)S(1)}, u32[]{:S(2)}, u32[]{:S(2)}) async-start(bf16[32,8,512]{2,1,0:T(8,128)(2,1)} %fusion.9), calls=%async_computation.1 | async-start | bytes 524288 | tf_op jit(solution)/shard_map/all_to_all | solution.py:101
  184.2 2.9 fusion.72
  188.9 3.4 fusion.44
  192.3 67.6 %all-reduce.7.cloned.1.call-done = bf16[256,3072]{1,0:T(8,128)(2,1)} async-done(((bf16[256,3072]{1,0:T(8,128)(2,1)}), bf16[256,3072]{1,0:T(8,128)(2,1)}) %all-reduce.7.cloned.1.call-update) | async-done | bytes 1572880 | tf_op jit(solution)/shard_map/psum | solution.py:80
  264.3 2.8 fusion.66
  267.0 2.7 fusion.68
  269.8 2.8 fusion.45
  272.6 74.8 %all-reduce.9.cloned.1.call-done = bf16[256,3072]{1,0:T(8,128)(2,1)} async-done(((bf16[256,3072]{1,0:T(8,128)(2,1)}), bf16[256,3072]{1,0:T(8,128)(2,1)}) %all-reduce.9.cloned.1.call-update) | async-done | bytes 1572880 | tf_op jit(solution)/shard_map/psum | solution.py:80
  350.4 2.7 fusion.62
  353.1 2.7 fusion.60
  357.1 2.9 fusion.46
  360.0 74.2 %all-reduce.11.cloned.1.call-done = bf16[256,3072]{1,0:T(8,128)(2,1)} async-done(((bf16[256,3072]{1,0:T(8,128)(2,1)}), bf16[256,3072]{1,0:T(8,128)(2,1)}) %all-reduce.11.cloned.1.call-update) | async-done | bytes 1572880 | tf_op jit(solution)/shard_map/psum | solution.py:80
  434.2 3.4 convert_element_type.120
  437.6 10.0 %all-to-all-start.3 = ((bf16[32,8,512]{2,1,0:T(8,128)(2,1)}), bf16[32,8,512]{2,1,0:T(8,128)(2,1)}, u32[]{:S(2)}, u32[]{:S(2)}) async-start(bf16[32,8,512]{2,1,0:T(8,128)(2,1)} %fusion.8), calls=%async_computation.3 | async-start | bytes 524288 | tf_op jit(solution)/shard_map/all_to_all | solution.py:101
  447.6 2.5 multiply_convert_fusion.4
  451.4 9.4 %all-to-all-done.3 = bf16[32,8,512]{2,1,0:T(8,128)(2,1)} async-done(((bf16[32,8,512]{2,1,0:T(8,128)(2,1)}), bf16[32,8,512]{2,1,0:T(8,128)(2,1)}, u32[]{:S(2)}, u32[]{:S(2)}) %all-to-all-start.3) | async-done | bytes 262176 | tf_op jit(solution)/shard_map/all_to_all | solution.py:101
  460.8 4.6 all-to-all-start.5
  467.1 4.5 add_bitcast_fusion.1
  471.5 6.7 %all-to-all-done.5 = bf16[32,8,512]{2,1,0:T(8,128)(2,1)} async-done(((bf16[32,8,512]{2,1,0:T(8,128)(2,1)}), bf16[32,8,512]{2,1,0:T(8,128)(2,1)}, u32[]{:S(2)}, u32[]{:S(2)}) %all-to-all-start.5) | async-done | bytes 262176 | tf_op jit(solution)/shard_map/all_to_all | solution.py:101
  478.2 4.6 all-to-all-start.7
  482.9 4.4 add_bitcast_fusion.2
  487.8 3.6 add_bitcast_fusion
  491.4 4.6 all-to-all-done.7
  (103 shorter events, 64.5 us)
Async XLA Ops:
  7.2 44.2 %copy-start = (bf16[1,512,1024]{2,1,0:T(8,128)(2,1)S(1)}, bf16[1,512,1024]{2,1,0:T(8,128)(2,1)}, u32[]{:S(2)}) copy-start(bf16[1,512,1024]{2,1,0:T(8,128)(2,1)} %param.11) | copy-start | bytes 3145732
  15.6 33.4 %copy-start.20 = (s32[256,2]{0,1:T(2,128)S(1)}, s32[256,2]{0,1:T(2,128)}, u32[]{:S(2)}) copy-start(s32[256,2]{0,1:T(2,128)} %param.9) | copy-start | bytes 6148
  15.6 33.5 %copy-start.1 = (bf16[1,512,1024]{2,1,0:T(8,128)(2,1)S(1)}, bf16[1,512,1024]{2,1,0:T(8,128)(2,1)}, u32[]{:S(2)}) copy-start(bf16[1,512,1024]{2,1,0:T(8,128)(2,1)} %param.12) | copy-start | bytes 3145732
  43.7 23.5 %all-to-all-start.2 = ((bf16[32,8,1024]{2,1,0:T(8,128)(2,1)}), bf16[32,8,1024]{2,1,0:T(8,128)(2,1)}, u32[]{:S(2)}, u32[]{:S(2)}) async-start(bf16[32,8,1024]{2,1,0:T(8,128)(2,1)} %get-tuple-element.23), calls=%async_computation.2 | async-start | bytes 1048576 | tf_op jit(solution)/shard_map/all_to_all | solution.py:61
  49.1 22.9 %copy-start.2 = (bf16[1,1024,512]{2,1,0:T(8,128)(2,1)S(1)}, bf16[1,1024,512]{2,1,0:T(8,128)(2,1)}, u32[]{:S(2)}) copy-start(bf16[1,1024,512]{2,1,0:T(8,128)(2,1)} %param.13) | copy-start | bytes 3145732
  67.3 22.9 %all-to-all-start.4 = ((bf16[32,8,1024]{2,1,0:T(8,128)(2,1)}), bf16[32,8,1024]{2,1,0:T(8,128)(2,1)}, u32[]{:S(2)}, u32[]{:S(2)}) async-start(bf16[32,8,1024]{2,1,0:T(8,128)(2,1)} %get-tuple-element.22), calls=%async_computation.4 | async-start | bytes 1048576 | tf_op jit(solution)/shard_map/all_to_all | solution.py:61
  71.9 97.0 %all-reduce.5.cloned.1.call-start = ((), (), s32[]{:S(2)}) async-start(), calls=%async_computation.8 | async-start | bytes 3145728 | tf_op jit(solution)/shard_map/psum | solution.py:80
  72.0 1.5 copy-start.17
  72.0 1.5 copy-start.18
  90.2 27.2 %all-to-all-start.6 = ((bf16[32,8,1024]{2,1,0:T(8,128)(2,1)}), bf16[32,8,1024]{2,1,0:T(8,128)(2,1)}, u32[]{:S(2)}, u32[]{:S(2)}) async-start(bf16[32,8,1024]{2,1,0:T(8,128)(2,1)} %get-tuple-element.21), calls=%async_computation.6 | async-start | bytes 1048576 | tf_op jit(solution)/shard_map/all_to_all | solution.py:61
  94.8 165.1 %all-reduce.7.cloned.1.call-start = ((), (), s32[]{:S(2)}) async-start(), calls=%async_computation.9 | async-start | bytes 3145728 | tf_op jit(solution)/shard_map/psum | solution.py:80
  119.6 4.6 copy-start.13
  119.6 4.6 copy-start.14
  119.6 4.6 copy-start.19
  121.9 3.5 copy-start.15
  121.9 3.5 copy-start.16
  170.7 1.6 copy-start.3
  172.3 0.8 copy-start.9
  172.3 11.9 %copy-start.6 = (bf16[32,8,1024]{2,1,0:T(8,128)(2,1)S(1)}, bf16[32,8,1024]{2,1,0:T(8,128)(2,1)}, u32[]{:S(2)}) copy-start(bf16[32,8,1024]{2,1,0:T(8,128)(2,1)} %all_to_all.40) | copy-start | bytes 1572868
  174.3 263.3 %all-to-all-start.1 = ((bf16[32,8,512]{2,1,0:T(8,128)(2,1)}), bf16[32,8,512]{2,1,0:T(8,128)(2,1)S(1)}, u32[]{:S(2)}, u32[]{:S(2)}) async-start(bf16[32,8,512]{2,1,0:T(8,128)(2,1)} %fusion.9), calls=%async_computation.1 | async-start | bytes 524288 | tf_op jit(solution)/shard_map/all_to_all | solution.py:101
  184.1 163.3 %all-reduce.9.cloned.1.call-start = ((), (), s32[]{:S(2)}) async-start(), calls=%async_computation.10 | async-start | bytes 3145728 | tf_op jit(solution)/shard_map/psum | solution.py:80
  259.9 174.3 %all-reduce.11.cloned.1.call-start = ((), (), s32[]{:S(2)}) async-start(), calls=%async_computation.11 | async-start | bytes 3145728 | tf_op jit(solution)/shard_map/psum | solution.py:80
  437.6 23.2 %all-to-all-start.3 = ((bf16[32,8,512]{2,1,0:T(8,128)(2,1)}), bf16[32,8,512]{2,1,0:T(8,128)(2,1)}, u32[]{:S(2)}, u32[]{:S(2)}) async-start(bf16[32,8,512]{2,1,0:T(8,128)(2,1)} %fusion.8), calls=%async_computation.3 | async-start | bytes 524288 | tf_op jit(solution)/shard_map/all_to_all | solution.py:101
  450.1 0.8 copy-start.7
  450.1 15.3 %copy-start.8 = (bf16[256,1024]{1,0:T(8,128)(2,1)}, bf16[256,1024]{1,0:T(8,128)(2,1)S(1)}, u32[]{:S(2)}) copy-start(bf16[256,1024]{1,0:T(8,128)(2,1)S(1)} %get-tuple-element.18) | copy-start | bytes 1572868
  460.8 17.4 %all-to-all-start.5 = ((bf16[32,8,512]{2,1,0:T(8,128)(2,1)}), bf16[32,8,512]{2,1,0:T(8,128)(2,1)}, u32[]{:S(2)}, u32[]{:S(2)}) async-start(bf16[32,8,512]{2,1,0:T(8,128)(2,1)} %fusion.7), calls=%async_computation.5 | async-start | bytes 524288 | tf_op jit(solution)/shard_map/all_to_all | solution.py:101
  465.4 1.7 copy-start.5
  467.1 15.7 %copy-start.4 = (f32[512,1024]{1,0:T(8,128)S(1)}, f32[512,1024]{1,0:T(8,128)}, u32[]{:S(2)}) copy-start(f32[512,1024]{1,0:T(8,128)} %fusion.74) | copy-start | bytes 6291460
  478.2 17.8 %all-to-all-start.7 = ((bf16[32,8,512]{2,1,0:T(8,128)(2,1)}), bf16[32,8,512]{2,1,0:T(8,128)(2,1)}, u32[]{:S(2)}, u32[]{:S(2)}) async-start(bf16[32,8,512]{2,1,0:T(8,128)(2,1)} %fusion.6), calls=%async_computation.7 | async-start | bytes 524288 | tf_op jit(solution)/shard_map/all_to_all | solution.py:101
  482.8 4.4 copy-start.10
  482.8 4.4 copy-start.11
  482.9 4.9 copy-start.12
Sparse Core Ops, SparseCore 0:
  76.0 92.8 all-reduce.4
  172.1 87.7 all-reduce.6
  263.2 84.2 all-reduce.8
  349.9 84.2 all-reduce.10

commit v2 on v0

--- a/solution.py
+++ b/solution.py
@@ -39,20 +39,15 @@
     scaled = (gate_probs.T.reshape(-1)[:, None] * grad_pick.astype(jnp.float32)).astype(
         jnp.bfloat16
     )
-    send_tokens = (
-        jnp.dot(placing, row_pick, preferred_element_type=jnp.float32)
+    both = jnp.concatenate([row_pick, scaled], axis=1)
+    send = (
+        jnp.dot(placing, both, preferred_element_type=jnp.float32)
         .astype(jnp.bfloat16)
-        .reshape(experts, MOST, slab_width)
+        .reshape(experts, MOST, 2 * slab_width)
     )
-    send_grads = (
-        jnp.dot(placing, scaled, preferred_element_type=jnp.float32)
-        .astype(jnp.bfloat16)
-        .reshape(experts, MOST, slab_width)
-    )
-    arrived_tokens, arrived_grads = (
-        lax.all_to_all(send_tokens, "expert", split_axis=0, concat_axis=0, tiled=True),
-        lax.all_to_all(send_grads, "expert", split_axis=0, concat_axis=0, tiled=True),
-    )
+    arrived = lax.all_to_all(send, "expert", split_axis=0, concat_axis=0, tiled=True)
+    arrived_tokens = arrived[:, :, :slab_width]
+    arrived_grads = arrived[:, :, slab_width:]
     flat_tokens = arrived_tokens.reshape(-1, slab_width)
     flat_grads = arrived_grads.reshape(-1, slab_width)
     gate_mat = w_gate[0]
@@ -68,7 +63,7 @@
         lax.psum(part_up.astype(jnp.bfloat16), "dp").astype(jnp.float32),
         lax.psum(part_act.astype(jnp.bfloat16), "dp").astype(jnp.float32),
     )
-    hidden, grad_gate, grad_up = local_grads(pre_gate, pre_up, grad_act)
+    hidden, grad_gate, grad_up = lax.optimization_barrier(local_grads(pre_gate, pre_up, grad_act))
     slot_grad = lax.dot_general(
         grad_gate, gate_mat, contract_cols, preferred_element_type=jnp.float32
     )
@@ -90,9 +85,9 @@
         split_axis=0,
         concat_axis=0,
         tiled=True,
-    ).astype(jnp.float32)
+    )
     flat_back = returned.reshape(experts * MOST, slab_width)
-    per_pick = jnp.take(flat_back, slot_of, axis=0)
+    per_pick = lax.dot_general(placing, flat_back, contract_rows, preferred_element_type=jnp.float32)
     token_grad = (per_pick[:tok_rows] + per_pick[tok_rows:]).astype(jnp.bfloat16)
     return (token_grad, gate_grads, up_grads, down_grads)
 

time: 299 us -> 290 us (0.970)
  blocking collectives: 0 us -> 61.8 us
  waiting for transfers between devices: 218 us -> 166 us
  starting transfers between devices: 25.6 us -> 10.1 us
    all_to_all x0 -> x1, blocking collectives: none -> 61.8 us  [shards(): lax.all_to_all(send, 'expert', split_axis=0, concat_axis=0, tiled=True)]
    all_to_all x2 -> x0, waiting for transfers between devices: 45.1 us -> none  [the longest x1 27.1 us: shards(): lax.all_to_all(send_tokens, 'expert', split_axis=0, concat_axis=0, tiled=...]
    all_to_all x2 -> x0, starting transfers between devices: 15.2 us -> none  [the longest x1 10.6 us: shards(): lax.all_to_all(send_tokens, 'expert', split_axis=0, concat_axis=0, tiled=...]
    psum x1, waiting for transfers between devices: 153 us -> 146 us  [shards(): lax.psum(part_up.astype(jnp.bfloat16), 'dp').astype(jnp.float32)]
  transfers between devices with their start and end apart: 4 -> 2, of which waited for: 4 -> 2; matrix products, arithmetic and copies ran while one was open for 6% -> 3% of each run, Pallas kernels for 0% -> 0%
where the time goes in v2:
time: 290 us
  waiting for transfers between devices  166 us (57%)
  blocking collectives  61.8 us (21%)
  matrix products  23.9 us (8%)
  between operations  14.1 us (5%)
  starting transfers between devices  10.1 us (3%)
  other arithmetic  8.84 us (3%)
  local copies, waits for them, and re-layouts  4.52 us (2%)
    psum x1, waiting for transfers between devices, shards(): lax.psum(part_up.astype(jnp.bfloat16), 'dp').astype(jnp.float32)  146 us
    all_to_all x1, blocking collectives, shards(): lax.all_to_all(send, 'expert', split_axis=0, concat_axis=0, tiled=True)  61.8 us
    all_to_all x1, waiting for transfers between devices, shards(): lax.all_to_all(slot_grad.reshape(experts, MOST, slab_width).astype(jnp.bf...  20.1 us
    all_to_all x1, starting transfers between devices, shards(): lax.all_to_all(slot_grad.reshape(experts, MOST, slab_width).astype(jnp.bf...  10 us
  transfers between devices with their start and end apart: 2, of which 2 were waited for; matrix products, arithmetic and copies ran while one was open for 3% of the time, Pallas kernels for 0%

profile of v2, /device:TPU:32, one launch (start us, length us, event | category | flops | bytes accessed | tf_op | source)
XLA Modules:
  0.0 289.6 jit_solution(15816448427289092793)
XLA Ops:
  7.2 0.0 copy-start
  7.2 0.0 all-reduce.3.cloned.1.call-start
  7.2 0.8 copy.14
  8.0 0.7 eq.40
  8.7 0.7 copy.13
  9.4 1.2 reduce-window.6
  10.5 0.2 slice_reduce_fusion
  10.8 0.1 fusion.27
  10.9 1.2 multiply_convert_fusion
  12.1 2.3 fusion.11
  14.4 61.8 %all_to_all.10 = bf16[32,32,1024]{2,1,0:T(8,128)(2,1)S(1)} all-to-all(bf16[32,32,1024]{2,1,0:T(8,128)(2,1)S(1)} %bitcast.61), channel_id=1, replica_groups=mesh['dp'=8,'expert'=32] {'expert'}, dimensions={0} | all-to-all | bytes 4194304 | tf_op jit(solution)/shard_map/all_to_all | solution.py:48
  76.3 0.2 fusion.30
  76.5 0.0 copy-start.5
  76.5 1.2 copy-done.8
  77.7 2.6 convolution_convert_fusion.1
  80.3 2.6 convolution_convert_fusion.2
  82.8 2.6 convolution_convert_fusion
  85.5 0.0 all-reduce.3.cloned.1.call-update
  85.5 146.2 %all-reduce.3.cloned.1.call-done = (bf16[1024,1024]{1,0:T(8,128)(2,1)}, bf16[1024,1024]{1,0:T(8,128)(2,1)}, bf16[1024,1024]{1,0:T(8,128)(2,1)}) async-done(((bf16[1024,1024]{1,0:T(8,128)(2,1)}, bf16[1024,1024]{1,0:T(8,128)(2,1)}, bf16[1024,1024]{1,0:T(8,128)(2,1)}), (bf16[1024,1024]{1,0:T(8,128)(2,1)}, bf16[1024,1024]{1,0:T(8,128)(2,1)}, bf16[1024,1024]{1,0:T(8,128)(2,1)})) %all-reduce.3.cloned.1.call-update) | async-done | bytes 6291472 | tf_op jit(solution)/shard_map/psum | solution.py:63
  231.7 5.5 %fusion.3 = (bf16[1024,1024]{1,0:T(8,128)(2,1)S(1)}, bf16[1024,1024]{1,0:T(8,128)(2,1)S(1)}, bf16[1024,1024]{1,0:T(8,128)(2,1)}) fusion(bf16[1024,1024]{1,0:T(8,128)(2,1)} %get-tuple-element.12, bf16[1024,1024]{1,0:T(8,128)(2,1)} %get-tuple-element.11, bf16[1024,1024]{1,0:T(8,128)(2,1)} %get-tuple-element.10), kind=kLoop, calls=%fused_computation.9 | loop fusion | flops 18874368 | bytes 12582912 | tf_op jit(solution)/shard_map/convert_element_type | solution.py:22
  237.2 1.3 fusion.20
  238.5 0.0 copy-done.1
  238.6 0.7 copy-done.3
  239.2 2.3 add_convert_fusion
  241.5 10.0 %all-to-all-start.1 = ((bf16[32,32,512]{2,1,0:T(8,128)(2,1)}), bf16[32,32,512]{2,1,0:T(8,128)(2,1)S(1)}, u32[]{:S(2)}, u32[]{:S(2)}) async-start(bf16[32,32,512]{2,1,0:T(8,128)(2,1)} %bitcast.63), calls=%async_computation.1 | async-start | bytes 2097152 | tf_op jit(solution)/shard_map/all_to_all | solution.py:82
  251.6 4.3 %convolution_bitcast_fusion.2 = f32[1,512,1024]{2,1,0:T(8,128)} fusion(bf16[1024,512]{1,0:T(8,128)(2,1)S(1)} %bitcast.59, bf16[1024,1024]{1,0:T(8,128)(2,1)} %copy-done.3), kind=kOutput, calls=%fused_computation.25 | convolution fusion | flops 1073741824 | bytes 5242880 | tf_op jit(solution)/shard_map/dot_general | solution.py:73
  255.9 2.6 convolution_bitcast_fusion.1
  258.5 0.0 copy-done.6
  258.5 2.6 convolution_bitcast_fusion
  261.1 20.1 %all-to-all-done.1 = bf16[32,32,512]{2,1,0:T(8,128)(2,1)S(1)} async-done(((bf16[32,32,512]{2,1,0:T(8,128)(2,1)}), bf16[32,32,512]{2,1,0:T(8,128)(2,1)S(1)}, u32[]{:S(2)}, u32[]{:S(2)}) %all-to-all-start.1) | async-done | bytes 1048608 | tf_op jit(solution)/shard_map/all_to_all | solution.py:82
  281.3 0.8 fusion.9
  282.0 0.8 fusion.25
  (16 shorter events, 0.1 us)
Async XLA Ops:
  7.2 73.1 %copy-start = (bf16[1,512,1024]{2,1,0:T(8,128)(2,1)S(1)}, bf16[1,512,1024]{2,1,0:T(8,128)(2,1)}, u32[]{:S(2)}) copy-start(bf16[1,512,1024]{2,1,0:T(8,128)(2,1)} %param.11) | copy-start | bytes 3145732
  7.2 224.5 %all-reduce.3.cloned.1.call-start = ((), (), s32[]{:S(2)}) async-start(), calls=%async_computation.2 | async-start | bytes 12582912 | tf_op jit(solution)/shard_map/psum | solution.py:63
  76.3 1.4 copy-start.8
  76.5 6.4 %copy-start.5 = (bf16[32,32,512]{2,1,0:T(8,128)(2,1)}, bf16[32,32,512]{2,1,0:T(8,128)(2,1)S(1)}, u32[]{:S(2)}) copy-start(bf16[32,32,512]{2,1,0:T(8,128)(2,1)S(1)} %get-tuple-element.16) | copy-start | bytes 3145732
  80.3 2.6 copy-start.7
  237.2 1.3 copy-start.1
  237.2 2.0 copy-start.3
  241.5 39.7 %all-to-all-start.1 = ((bf16[32,32,512]{2,1,0:T(8,128)(2,1)}), bf16[32,32,512]{2,1,0:T(8,128)(2,1)S(1)}, u32[]{:S(2)}, u32[]{:S(2)}) async-start(bf16[32,32,512]{2,1,0:T(8,128)(2,1)} %bitcast.63), calls=%async_computation.1 | async-start | bytes 2097152 | tf_op jit(solution)/shard_map/all_to_all | solution.py:82
  251.6 4.3 %copy-start.2 = (bf16[1024,1024]{1,0:T(8,128)(2,1)S(1)}, bf16[1024,1024]{1,0:T(8,128)(2,1)}, u32[]{:S(2)}) copy-start(bf16[1024,1024]{1,0:T(8,128)(2,1)} %copy-done.1) | copy-start | bytes 6291460
  255.9 2.6 copy-start.4
  255.9 2.6 copy-start.6
Sparse Core Ops, SparseCore 0:
  85.6 146.0 all-reduce.2

commit v3 on v2

--- a/solution.py
+++ b/solution.py
@@ -63,7 +63,8 @@
         lax.psum(part_up.astype(jnp.bfloat16), "dp").astype(jnp.float32),
         lax.psum(part_act.astype(jnp.bfloat16), "dp").astype(jnp.float32),
     )
-    hidden, grad_gate, grad_up = lax.optimization_barrier(local_grads(pre_gate, pre_up, grad_act))
+    hidden, grad_gate, grad_up = local_grads(pre_gate, pre_up, grad_act)
+    grad_gate, grad_up = lax.optimization_barrier((grad_gate, grad_up))
     slot_grad = lax.dot_general(
         grad_gate, gate_mat, contract_cols, preferred_element_type=jnp.float32
     )

time: 290 us -> 287 us (0.990)
  no operation moved by 1% of the time
where the time goes in v3:
time: 287 us
  waiting for transfers between devices  166 us (58%)
  blocking collectives  61.8 us (22%)
  matrix products  24.1 us (8%)
  between operations  14.2 us (5%)
  starting transfers between devices  10.1 us (4%)
  other arithmetic  7.53 us (3%)
  local copies, waits for them, and re-layouts  3.88 us (1%)
    psum x1, waiting for transfers between devices, shards(): lax.psum(part_up.astype(jnp.bfloat16), 'dp').astype(jnp.float32)  146 us
    all_to_all x1, blocking collectives, shards(): lax.all_to_all(send, 'expert', split_axis=0, concat_axis=0, tiled=True)  61.8 us
    all_to_all x1, waiting for transfers between devices, shards(): lax.all_to_all(slot_grad.reshape(experts, MOST, slab_width).astype(jnp.bf...  19.3 us
    all_to_all x1, starting transfers between devices, shards(): lax.all_to_all(slot_grad.reshape(experts, MOST, slab_width).astype(jnp.bf...  10 us
  transfers between devices with their start and end apart: 2, of which 2 were waited for; matrix products, arithmetic and copies ran while one was open for 3% of the time, Pallas kernels for 0%

profile of v3, /device:TPU:32, one launch (start us, length us, event | category | flops | bytes accessed | tf_op | source)
XLA Modules:
  0.0 287.1 jit_solution(2326198990944406532)
XLA Ops:
  7.2 0.0 copy-start
  7.2 0.0 all-reduce.3.cloned.1.call-start
  7.2 0.8 copy.14
  8.0 0.7 eq.40
  8.7 0.7 copy.13
  9.4 1.2 reduce-window.6
  10.5 0.2 slice_reduce_fusion
  10.8 0.1 fusion.32
  10.9 1.2 multiply_convert_fusion
  12.1 2.3 fusion.13
  14.4 61.8 %all_to_all.10 = bf16[32,32,1024]{2,1,0:T(8,128)(2,1)S(1)} all-to-all(bf16[32,32,1024]{2,1,0:T(8,128)(2,1)S(1)} %bitcast.60), channel_id=1, replica_groups=mesh['dp'=8,'expert'=32] {'expert'}, dimensions={0} | all-to-all | bytes 4194304 | tf_op jit(solution)/shard_map/all_to_all | solution.py:48
  76.3 0.2 fusion.36
  76.5 0.0 copy-start.9
  76.5 2.6 convolution_convert_fusion
  79.1 2.6 convolution_convert_fusion.1
  81.7 2.6 convolution_convert_fusion.2
  84.3 0.0 all-reduce.3.cloned.1.call-update
  84.3 146.2 %all-reduce.3.cloned.1.call-done = (bf16[1024,1024]{1,0:T(8,128)(2,1)}, bf16[1024,1024]{1,0:T(8,128)(2,1)}, bf16[1024,1024]{1,0:T(8,128)(2,1)}) async-done(((bf16[1024,1024]{1,0:T(8,128)(2,1)}, bf16[1024,1024]{1,0:T(8,128)(2,1)}, bf16[1024,1024]{1,0:T(8,128)(2,1)}), (bf16[1024,1024]{1,0:T(8,128)(2,1)}, bf16[1024,1024]{1,0:T(8,128)(2,1)}, bf16[1024,1024]{1,0:T(8,128)(2,1)})) %all-reduce.3.cloned.1.call-update) | async-done | bytes 6291472 | tf_op jit(solution)/shard_map/psum | solution.py:63
  230.5 4.2 %fusion = (bf16[1024,1024]{1,0:T(8,128)(2,1)S(1)}, bf16[1024,1024]{1,0:T(8,128)(2,1)S(1)}) fusion(bf16[1024,1024]{1,0:T(8,128)(2,1)} %get-tuple-element.9, bf16[1024,1024]{1,0:T(8,128)(2,1)} %get-tuple-element.10, bf16[1024,1024]{1,0:T(8,128)(2,1)} %get-tuple-element.8), kind=kLoop, calls=%fused_computation.6 | loop fusion | flops 16777216 | bytes 10485760 | tf_op jit(solution)/shard_map/convert_element_type | solution.py:22
  234.7 0.0 copy-start.1
  234.7 1.3 fusion.22
  236.0 0.0 copy-done.1
  236.0 0.7 copy-done.3
  236.7 2.3 add_convert_fusion
  239.0 10.0 %all-to-all-start.1 = ((bf16[32,32,512]{2,1,0:T(8,128)(2,1)}), bf16[32,32,512]{2,1,0:T(8,128)(2,1)S(1)}, u32[]{:S(2)}, u32[]{:S(2)}) async-start(bf16[32,32,512]{2,1,0:T(8,128)(2,1)} %bitcast.62), calls=%async_computation.1 | async-start | bytes 2097152 | tf_op jit(solution)/shard_map/all_to_all | solution.py:83
  249.1 4.3 %convolution_bitcast_fusion.1 = f32[1,512,1024]{2,1,0:T(8,128)} fusion(bf16[1024,512]{1,0:T(8,128)(2,1)S(1)} %bitcast.58, bf16[1024,1024]{1,0:T(8,128)(2,1)} %copy-done.3), kind=kOutput, calls=%fused_computation.26 | convolution fusion | flops 1073741824 | bytes 5242880 | tf_op jit(solution)/shard_map/dot_general | solution.py:74
  253.4 2.6 convolution_bitcast_fusion
  256.0 0.6 copy-done.7
  256.6 2.8 fusion.14
  259.4 19.3 %all-to-all-done.1 = bf16[32,32,512]{2,1,0:T(8,128)(2,1)S(1)} async-done(((bf16[32,32,512]{2,1,0:T(8,128)(2,1)}), bf16[32,32,512]{2,1,0:T(8,128)(2,1)S(1)}, u32[]{:S(2)}, u32[]{:S(2)}) %all-to-all-start.1) | async-done | bytes 1048608 | tf_op jit(solution)/shard_map/all_to_all | solution.py:83
  278.7 0.8 fusion.11
  279.5 0.8 fusion.30
  (18 shorter events, 0.1 us)
Async XLA Ops:
  7.2 69.3 %copy-start = (bf16[1,512,1024]{2,1,0:T(8,128)(2,1)S(1)}, bf16[1,512,1024]{2,1,0:T(8,128)(2,1)}, u32[]{:S(2)}) copy-start(bf16[1,512,1024]{2,1,0:T(8,128)(2,1)} %param.11) | copy-start | bytes 3145732
  7.2 223.3 %all-reduce.3.cloned.1.call-start = ((), (), s32[]{:S(2)}) async-start(), calls=%async_computation.2 | async-start | bytes 12582912 | tf_op jit(solution)/shard_map/psum | solution.py:63
  76.5 5.2 %copy-start.6 = (bf16[32,32,512]{2,1,0:T(8,128)(2,1)}, bf16[32,32,512]{2,1,0:T(8,128)(2,1)S(1)}, u32[]{:S(2)}) copy-start(bf16[32,32,512]{2,1,0:T(8,128)(2,1)S(1)} %get-tuple-element.13) | copy-start | bytes 3145732
  76.5 2.6 copy-start.9
  79.1 2.6 copy-start.8
  234.7 1.3 copy-start.1
  234.7 2.0 copy-start.3
  239.0 39.7 %all-to-all-start.1 = ((bf16[32,32,512]{2,1,0:T(8,128)(2,1)}), bf16[32,32,512]{2,1,0:T(8,128)(2,1)S(1)}, u32[]{:S(2)}, u32[]{:S(2)}) async-start(bf16[32,32,512]{2,1,0:T(8,128)(2,1)} %bitcast.62), calls=%async_computation.1 | async-start | bytes 2097152 | tf_op jit(solution)/shard_map/all_to_all | solution.py:83
  249.0 4.3 %copy-start.2 = (bf16[1024,1024]{1,0:T(8,128)(2,1)S(1)}, bf16[1024,1024]{1,0:T(8,128)(2,1)}, u32[]{:S(2)}) copy-start(bf16[1024,1024]{1,0:T(8,128)(2,1)} %copy-done.1) | copy-start | bytes 6291460
  253.4 2.6 copy-start.4
  253.4 2.6 copy-start.5
  253.4 3.2 %copy-start.7 = (bf16[32,32,512]{2,1,0:T(8,128)(2,1)S(1)}, bf16[32,32,512]{2,1,0:T(8,128)(2,1)}, u32[]{:S(2)}) copy-start(bf16[32,32,512]{2,1,0:T(8,128)(2,1)} %copy-done.6) | copy-start | bytes 3145732
Sparse Core Ops, SparseCore 0:
  84.4 146.0 all-reduce.2

commit v4 on v3

--- a/solution.py
+++ b/solution.py
@@ -59,9 +59,9 @@
         flat_grads, down_mat, contract_cols, preferred_element_type=jnp.float32
     )
     pre_gate, pre_up, grad_act = (
-        lax.psum(part_gate.astype(jnp.bfloat16), "dp").astype(jnp.float32),
-        lax.psum(part_up.astype(jnp.bfloat16), "dp").astype(jnp.float32),
-        lax.psum(part_act.astype(jnp.bfloat16), "dp").astype(jnp.float32),
+        lax.psum(part_gate, "dp"),
+        lax.psum(part_up, "dp"),
+        lax.psum(part_act, "dp"),
     )
     hidden, grad_gate, grad_up = local_grads(pre_gate, pre_up, grad_act)
     grad_gate, grad_up = lax.optimization_barrier((grad_gate, grad_up))

time: 287 us -> 410 us (1.43)
  waiting for transfers between devices: 166 us -> 284 us
    psum x1, waiting for transfers between devices: 146 us -> 265 us  [shards(): lax.psum(part_gate, 'dp')]
where the time goes in v4:
time: 410 us; the launch traced here: 409 us
  waiting for transfers between devices  284 us (69%)
  blocking collectives  61.8 us (15%)
  matrix products  27.2 us (7%)
  between operations  14.2 us (3%)
  starting transfers between devices  10.1 us (2%)
  other arithmetic  9.23 us (2%)
    psum x1, waiting for transfers between devices, shards(): lax.psum(part_gate, 'dp')  265 us
    all_to_all x1, blocking collectives, shards(): lax.all_to_all(send, 'expert', split_axis=0, concat_axis=0, tiled=True)  61.8 us
    all_to_all x1, waiting for transfers between devices, shards(): lax.all_to_all(slot_grad.reshape(experts, MOST, slab_width).astype(jnp.bf...  18.8 us
    all_to_all x1, starting transfers between devices, shards(): lax.all_to_all(slot_grad.reshape(experts, MOST, slab_width).astype(jnp.bf...  10 us
  transfers between devices with their start and end apart: 2, of which 2 were waited for; matrix products, arithmetic and copies ran while one was open for 3% of the time, Pallas kernels for 0%

profile of v4, /device:TPU:32, one launch (start us, length us, event | category | flops | bytes accessed | tf_op | source)
XLA Modules:
  0.0 409.3 jit_solution(17615021156421223449)
XLA Ops:
  7.2 0.0 copy-start
  7.2 0.0 all-reduce.3.cloned.1.call-start
  7.2 0.8 copy.14
  8.0 0.7 eq.40
  8.7 0.7 copy.13
  9.4 1.2 reduce-window.6
  10.5 0.2 slice_reduce_fusion
  10.8 0.1 fusion.25
  10.9 1.2 multiply_convert_fusion.6
  12.1 2.3 fusion.4
  14.4 61.8 %all_to_all.10 = bf16[32,32,1024]{2,1,0:T(8,128)(2,1)S(1)} all-to-all(bf16[32,32,1024]{2,1,0:T(8,128)(2,1)S(1)} %bitcast.60), channel_id=1, replica_groups=mesh['dp'=8,'expert'=32] {'expert'}, dimensions={0} | all-to-all | bytes 4194304 | tf_op jit(solution)/shard_map/all_to_all | solution.py:48
  76.2 0.2 fusion.29
  76.4 0.0 copy-start.8
  76.4 3.2 fusion.13
  79.6 3.2 fusion.16
  82.8 3.2 fusion.18
  86.1 0.0 all-reduce.3.cloned.1.call-update
  86.1 264.8 %all-reduce.3.cloned.1.call-done = (f32[1024,1024]{1,0:T(8,128)}, f32[1024,1024]{1,0:T(8,128)}, f32[1024,1024]{1,0:T(8,128)}) async-done(((f32[1024,1024]{1,0:T(8,128)}, f32[1024,1024]{1,0:T(8,128)}, f32[1024,1024]{1,0:T(8,128)}), (f32[1024,1024]{1,0:T(8,128)}, f32[1024,1024]{1,0:T(8,128)}, f32[1024,1024]{1,0:T(8,128)})) %all-reduce.3.cloned.1.call-update) | async-done | bytes 12582928 | tf_op jit(solution)/shard_map/psum | solution.py:62
  350.9 5.9 %multiply_convert_fusion.1 = (bf16[1024,1024]{1,0:T(8,128)(2,1)S(1)}, bf16[1024,1024]{1,0:T(8,128)(2,1)S(1)}) fusion(f32[1024,1024]{1,0:T(8,128)} %get-tuple-element.9, f32[1024,1024]{1,0:T(8,128)} %get-tuple-element.8, f32[1024,1024]{1,0:T(8,128)} %get-tuple-element.10), kind=kLoop, calls=%fused_computation.1 | loop fusion | flops 13631488 | bytes 16777216 | tf_op jit(solution)/shard_map/convert_element_type | solution.py:22
  356.8 0.0 copy-start.3
  356.9 1.3 fusion.11
  358.1 0.0 copy-done.1
  358.2 0.7 copy-done.3
  358.8 2.4 add_convert_fusion
  361.2 10.0 %all-to-all-start.1 = ((bf16[32,32,512]{2,1,0:T(8,128)(2,1)}), bf16[32,32,512]{2,1,0:T(8,128)(2,1)S(1)}, u32[]{:S(2)}, u32[]{:S(2)}) async-start(bf16[32,32,512]{2,1,0:T(8,128)(2,1)} %bitcast.62), calls=%async_computation.1 | async-start | bytes 2097152 | tf_op jit(solution)/shard_map/all_to_all | solution.py:83
  371.2 0.0 copy-start.2
  371.3 4.3 %convolution_bitcast_fusion.1 = f32[1,512,1024]{2,1,0:T(8,128)} fusion(bf16[1024,512]{1,0:T(8,128)(2,1)S(1)} %bitcast.58, bf16[1024,1024]{1,0:T(8,128)(2,1)} %copy-done.3), kind=kOutput, calls=%fused_computation.13 | convolution fusion | flops 1073741824 | bytes 5242880 | tf_op jit(solution)/shard_map/dot_general | solution.py:74
  375.6 2.6 convolution_bitcast_fusion
  378.2 3.9 fusion.5
  382.1 18.8 %all-to-all-done.1 = bf16[32,32,512]{2,1,0:T(8,128)(2,1)S(1)} async-done(((bf16[32,32,512]{2,1,0:T(8,128)(2,1)}), bf16[32,32,512]{2,1,0:T(8,128)(2,1)S(1)}, u32[]{:S(2)}, u32[]{:S(2)}) %all-to-all-start.1) | async-done | bytes 1048608 | tf_op jit(solution)/shard_map/all_to_all | solution.py:83
  400.9 0.8 fusion.2
  401.7 0.8 fusion.23
  (16 shorter events, 0.1 us)
Async XLA Ops:
  7.2 69.2 %copy-start = (bf16[1,512,1024]{2,1,0:T(8,128)(2,1)S(1)}, bf16[1,512,1024]{2,1,0:T(8,128)(2,1)}, u32[]{:S(2)}) copy-start(bf16[1,512,1024]{2,1,0:T(8,128)(2,1)} %param.11) | copy-start | bytes 3145732
  7.2 343.7 %all-reduce.3.cloned.1.call-start = ((), (), s32[]{:S(2)}) async-start(), calls=%async_computation.2 | async-start | bytes 25165824 | tf_op jit(solution)/shard_map/psum | solution.py:62
  76.4 6.5 %copy-start.6 = (bf16[32,32,512]{2,1,0:T(8,128)(2,1)}, bf16[32,32,512]{2,1,0:T(8,128)(2,1)S(1)}, u32[]{:S(2)}) copy-start(bf16[32,32,512]{2,1,0:T(8,128)(2,1)S(1)} %get-tuple-element.13) | copy-start | bytes 3145732
  76.4 3.2 copy-start.8
  79.6 3.2 copy-start.7
  356.8 1.3 copy-start.1
  356.8 2.0 copy-start.3
  361.2 39.7 %all-to-all-start.1 = ((bf16[32,32,512]{2,1,0:T(8,128)(2,1)}), bf16[32,32,512]{2,1,0:T(8,128)(2,1)S(1)}, u32[]{:S(2)}, u32[]{:S(2)}) async-start(bf16[32,32,512]{2,1,0:T(8,128)(2,1)} %bitcast.62), calls=%async_computation.1 | async-start | bytes 2097152 | tf_op jit(solution)/shard_map/all_to_all | solution.py:83
  371.2 4.4 %copy-start.2 = (bf16[1024,1024]{1,0:T(8,128)(2,1)S(1)}, bf16[1024,1024]{1,0:T(8,128)(2,1)}, u32[]{:S(2)}) copy-start(bf16[1024,1024]{1,0:T(8,128)(2,1)} %copy-done.1) | copy-start | bytes 6291460
  371.2 6.9 %copy-start.5 = (f32[1024,1024]{1,0:T(8,128)S(1)}, f32[1024,1024]{1,0:T(8,128)}, u32[]{:S(2)}) copy-start(f32[1024,1024]{1,0:T(8,128)} %get-tuple-element.10) | copy-start | bytes 12582916
  375.6 2.6 copy-start.4
Sparse Core Ops, SparseCore 0:
  86.2 264.6 all-reduce.2

commit v5 on v3

--- a/solution.py
+++ b/solution.py
@@ -53,8 +53,11 @@
     gate_mat = w_gate[0]
     up_mat = w_up[0]
     down_mat = w_down[0]
-    part_gate = jnp.dot(flat_tokens, gate_mat, preferred_element_type=jnp.float32)
-    part_up = jnp.dot(flat_tokens, up_mat, preferred_element_type=jnp.float32)
+    hidden_width = gate_mat.shape[1]
+    gate_up_mat = jnp.concatenate([gate_mat, up_mat], axis=1)
+    part_gate_up = jnp.dot(flat_tokens, gate_up_mat, preferred_element_type=jnp.float32)
+    part_gate = part_gate_up[:, :hidden_width]
+    part_up = part_gate_up[:, hidden_width:]
     part_act = lax.dot_general(
         flat_grads, down_mat, contract_cols, preferred_element_type=jnp.float32
     )
@@ -66,10 +69,10 @@
     hidden, grad_gate, grad_up = local_grads(pre_gate, pre_up, grad_act)
     grad_gate, grad_up = lax.optimization_barrier((grad_gate, grad_up))
     slot_grad = lax.dot_general(
-        grad_gate, gate_mat, contract_cols, preferred_element_type=jnp.float32
-    )
-    slot_grad = slot_grad + lax.dot_general(
-        grad_up, up_mat, contract_cols, preferred_element_type=jnp.float32
+        jnp.concatenate([grad_gate, grad_up], axis=1),
+        gate_up_mat,
+        contract_cols,
+        preferred_element_type=jnp.float32,
     )
     gate_grads = lax.dot_general(
         flat_tokens, grad_gate, contract_rows, preferred_element_type=jnp.float32

time: 287 us -> 288 us (level)
  local copies, waits for them, and re-layouts: 3.88 us -> 7.35 us
  matrix products: 24.1 us -> 21.1 us
    dot_general x4 -> x2, matrix products: 8.7 us -> 5.69 us  [the longest x1 3.34 us: shards(): lax.dot_general(jnp.concatenate([grad_gate, grad_up], axis=1), gate_up_ma...]
where the time goes in v5:
time: 288 us
  waiting for transfers between devices  166 us (58%)
  blocking collectives  61.8 us (21%)
  matrix products  21.1 us (7%)
  between operations  14.2 us (5%)
  starting transfers between devices  10.1 us (4%)
  other arithmetic  7.62 us (3%)
  local copies, waits for them, and re-layouts  7.35 us (3%)
    psum x1, waiting for transfers between devices, shards(): lax.psum(part_up.astype(jnp.bfloat16), 'dp').astype(jnp.float32)  146 us
    all_to_all x1, blocking collectives, shards(): lax.all_to_all(send, 'expert', split_axis=0, concat_axis=0, tiled=True)  61.8 us
    all_to_all x1, waiting for transfers between devices, shards(): lax.all_to_all(slot_grad.reshape(experts, MOST, slab_width).astype(jnp.bf...  19.3 us
    all_to_all x1, starting transfers between devices, shards(): lax.all_to_all(slot_grad.reshape(experts, MOST, slab_width).astype(jnp.bf...  10 us
  transfers between devices with their start and end apart: 2, of which 2 were waited for; matrix products, arithmetic and copies ran while one was open for 3% of the time, Pallas kernels for 0%

profile of v5, /device:TPU:32, one launch (start us, length us, event | category | flops | bytes accessed | tf_op | source)
XLA Modules:
  0.0 287.6 jit_solution(1551974871216572349)
XLA Ops:
  7.2 0.0 copy-start
  7.2 0.0 all-reduce.3.cloned.1.call-start
  7.2 0.8 copy.14
  8.0 0.7 eq.40
  8.7 0.7 copy.13
  9.4 1.2 reduce-window.6
  10.5 0.2 slice_reduce_fusion
  10.8 0.1 fusion.34
  10.9 1.2 multiply_convert_fusion
  12.1 2.3 fusion.17
  14.4 61.8 %all_to_all.10 = bf16[32,32,1024]{2,1,0:T(8,128)(2,1)S(1)} all-to-all(bf16[32,32,1024]{2,1,0:T(8,128)(2,1)S(1)} %bitcast.48), channel_id=1, replica_groups=mesh['dp'=8,'expert'=32] {'expert'}, dimensions={0} | all-to-all | bytes 4194304 | tf_op jit(solution)/shard_map/all_to_all | solution.py:48
  76.2 0.2 fusion.41
  76.4 1.3 copy-done.8
  77.7 0.4 copy-done.9
  78.1 2.3 convolution_convert_fusion
  80.5 2.5 fusion.40
  83.0 2.6 convolution_convert_fusion.1
  85.6 0.0 all-reduce.3.cloned.1.call-update
  85.6 146.2 %all-reduce.3.cloned.1.call-done = (bf16[1024,1024]{1,0:T(8,128)(2,1)}, bf16[1024,1024]{1,0:T(8,128)(2,1)}, bf16[1024,1024]{1,0:T(8,128)(2,1)}) async-done(((bf16[1024,1024]{1,0:T(8,128)(2,1)}, bf16[1024,1024]{1,0:T(8,128)(2,1)}, bf16[1024,1024]{1,0:T(8,128)(2,1)}), (bf16[1024,1024]{1,0:T(8,128)(2,1)}, bf16[1024,1024]{1,0:T(8,128)(2,1)}, bf16[1024,1024]{1,0:T(8,128)(2,1)})) %all-reduce.3.cloned.1.call-update) | async-done | bytes 6291472 | tf_op jit(solution)/shard_map/psum | solution.py:66
  231.8 4.3 %fusion = (bf16[1024,1024]{1,0:T(8,128)(2,1)S(1)}, bf16[1024,1024]{1,0:T(8,128)(2,1)S(1)}) fusion(bf16[1024,1024]{1,0:T(8,128)(2,1)} %get-tuple-element.9, bf16[1024,1024]{1,0:T(8,128)(2,1)} %get-tuple-element.10, bf16[1024,1024]{1,0:T(8,128)(2,1)} %get-tuple-element.8), kind=kLoop, calls=%fused_computation.6 | loop fusion | flops 16777216 | bytes 10485760 | tf_op jit(solution)/shard_map/convert_element_type | solution.py:22
  236.1 0.0 copy-start.1
  236.1 0.0 copy-start.3
  236.1 3.3 %fusion.21 = bf16[1024,512]{1,0:T(8,128)(2,1)} fusion(bf16[1024,1024]{1,0:T(8,128)(2,1)S(1)} %get-tuple-element.7, bf16[1024,1024]{1,0:T(8,128)(2,1)S(1)} %get-tuple-element.6, bf16[512,1024]{1,0:T(8,128)(2,1)S(1)} %bitcast.60, bf16[512,1024]{1,0:T(8,128)(2,1)S(1)} %bitcast.62), kind=kOutput, calls=%fused_computation.30 | convolution fusion | flops 2160590848 | bytes 7340032 | tf_op jit(solution)/shard_map/dot_general | solution.py:71
  239.5 10.0 %all-to-all-start.1 = ((bf16[32,32,512]{2,1,0:T(8,128)(2,1)}), bf16[32,32,512]{2,1,0:T(8,128)(2,1)S(1)}, u32[]{:S(2)}, u32[]{:S(2)}) async-start(bf16[32,32,512]{2,1,0:T(8,128)(2,1)} %bitcast.50), calls=%async_computation.1 | async-start | bytes 2097152 | tf_op jit(solution)/shard_map/all_to_all | solution.py:86
  249.5 0.0 copy-start.2
  249.5 4.3 %convolution_bitcast_fusion.1 = f32[1,512,1024]{2,1,0:T(8,128)} fusion(bf16[1024,512]{1,0:T(8,128)(2,1)S(1)} %bitcast.46, bf16[1024,1024]{1,0:T(8,128)(2,1)} %copy-done.3), kind=kOutput, calls=%fused_computation.29 | convolution fusion | flops 1073741824 | bytes 5242880 | tf_op jit(solution)/shard_map/dot_general | solution.py:77
  253.9 2.6 convolution_bitcast_fusion
  256.5 0.6 copy-done.7
  257.0 2.8 fusion.18
  259.9 19.3 %all-to-all-done.1 = bf16[32,32,512]{2,1,0:T(8,128)(2,1)S(1)} async-done(((bf16[32,32,512]{2,1,0:T(8,128)(2,1)}), bf16[32,32,512]{2,1,0:T(8,128)(2,1)S(1)}, u32[]{:S(2)}, u32[]{:S(2)}) %all-to-all-start.1) | async-done | bytes 1048608 | tf_op jit(solution)/shard_map/all_to_all | solution.py:86
  279.2 0.8 fusion.15
  280.0 0.8 fusion.32
  (19 shorter events, 0.1 us)
Async XLA Ops:
  7.2 75.8 %copy-start = (bf16[1,1024,512]{2,1,0:T(8,128)(2,1)S(1)}, bf16[1,1024,512]{2,1,0:T(8,128)(2,1)}, u32[]{:S(2)}) copy-start(bf16[1,1024,512]{2,1,0:T(8,128)(2,1)} %param.13) | copy-start | bytes 3145732
  7.2 224.6 %all-reduce.3.cloned.1.call-start = ((), (), s32[]{:S(2)}) async-start(), calls=%async_computation.2 | async-start | bytes 12582912 | tf_op jit(solution)/shard_map/psum | solution.py:66
  76.2 1.5 copy-start.8
  76.2 1.9 copy-start.9
  76.4 6.6 %copy-start.6 = (bf16[32,32,512]{2,1,0:T(8,128)(2,1)}, bf16[32,32,512]{2,1,0:T(8,128)(2,1)S(1)}, u32[]{:S(2)}) copy-start(bf16[32,32,512]{2,1,0:T(8,128)(2,1)S(1)} %get-tuple-element.15) | copy-start | bytes 3145732
  231.8 4.4 %copy-start.10 = (bf16[1,512,1024]{2,1,0:T(8,128)(2,1)S(1)}, bf16[1,512,1024]{2,1,0:T(8,128)(2,1)}, u32[]{:S(2)}) copy-start(bf16[1,512,1024]{2,1,0:T(8,128)(2,1)} %param.11) | copy-start | bytes 3145732
  236.1 3.4 %copy-start.1 = (bf16[1024,1024]{1,0:T(8,128)(2,1)}, bf16[1024,1024]{1,0:T(8,128)(2,1)S(1)}, u32[]{:S(2)}) copy-start(bf16[1024,1024]{1,0:T(8,128)(2,1)S(1)} %get-tuple-element.7) | copy-start | bytes 6291460
  236.1 3.4 %copy-start.3 = (bf16[1024,1024]{1,0:T(8,128)(2,1)}, bf16[1024,1024]{1,0:T(8,128)(2,1)S(1)}, u32[]{:S(2)}) copy-start(bf16[1024,1024]{1,0:T(8,128)(2,1)S(1)} %get-tuple-element.6) | copy-start | bytes 6291460
  239.5 39.7 %all-to-all-start.1 = ((bf16[32,32,512]{2,1,0:T(8,128)(2,1)}), bf16[32,32,512]{2,1,0:T(8,128)(2,1)S(1)}, u32[]{:S(2)}, u32[]{:S(2)}) async-start(bf16[32,32,512]{2,1,0:T(8,128)(2,1)} %bitcast.50), calls=%async_computation.1 | async-start | bytes 2097152 | tf_op jit(solution)/shard_map/all_to_all | solution.py:86
  249.5 4.3 %copy-start.2 = (bf16[1024,1024]{1,0:T(8,128)(2,1)S(1)}, bf16[1024,1024]{1,0:T(8,128)(2,1)}, u32[]{:S(2)}) copy-start(bf16[1024,1024]{1,0:T(8,128)(2,1)} %copy-done.1) | copy-start | bytes 6291460
  253.9 2.6 copy-start.4
  253.9 2.6 copy-start.5
  253.9 3.2 %copy-start.7 = (bf16[32,32,512]{2,1,0:T(8,128)(2,1)S(1)}, bf16[32,32,512]{2,1,0:T(8,128)(2,1)}, u32[]{:S(2)}) copy-start(bf16[32,32,512]{2,1,0:T(8,128)(2,1)} %copy-done.6) | copy-start | bytes 3145732
Sparse Core Ops, SparseCore 0:
  85.7 146.0 all-reduce.2

commit v6 on v5

--- a/solution.py
+++ b/solution.py
@@ -56,16 +56,16 @@
     hidden_width = gate_mat.shape[1]
     gate_up_mat = jnp.concatenate([gate_mat, up_mat], axis=1)
     part_gate_up = jnp.dot(flat_tokens, gate_up_mat, preferred_element_type=jnp.float32)
-    part_gate = part_gate_up[:, :hidden_width]
-    part_up = part_gate_up[:, hidden_width:]
     part_act = lax.dot_general(
         flat_grads, down_mat, contract_cols, preferred_element_type=jnp.float32
     )
-    pre_gate, pre_up, grad_act = (
-        lax.psum(part_gate.astype(jnp.bfloat16), "dp").astype(jnp.float32),
-        lax.psum(part_up.astype(jnp.bfloat16), "dp").astype(jnp.float32),
-        lax.psum(part_act.astype(jnp.bfloat16), "dp").astype(jnp.float32),
+    summed_gate_up, summed_act = lax.psum(
+        (part_gate_up.astype(jnp.bfloat16), part_act.astype(jnp.bfloat16)), "dp"
     )
+    wide = summed_gate_up.astype(jnp.float32)
+    pre_gate = wide[:, :hidden_width]
+    pre_up = wide[:, hidden_width:]
+    grad_act = summed_act.astype(jnp.float32)
     hidden, grad_gate, grad_up = local_grads(pre_gate, pre_up, grad_act)
     grad_gate, grad_up = lax.optimization_barrier((grad_gate, grad_up))
     slot_grad = lax.dot_general(

time: 288 us -> 288 us (level)
  local copies, waits for them, and re-layouts: 7.35 us -> 3.22 us
  matrix products: 21.1 us -> 24.5 us
    convert_element_type x0 -> x1, other arithmetic: none -> 3.41 us  [shards(): wide = summed_gate_up.astype(jnp.float32)]
  transfers between devices with their start and end apart: 2 -> 2, of which waited for: 2 -> 2; matrix products, arithmetic and copies ran while one was open for 3% -> 4% of each run, Pallas kernels for 0% -> 0%
where the time goes in v6:
time: 288 us
  waiting for transfers between devices  165 us (57%)
  blocking collectives  61.8 us (21%)
  matrix products  24.5 us (9%)
  between operations  14.2 us (5%)
  starting transfers between devices  10.1 us (4%)
  other arithmetic  9.31 us (3%)
  local copies, waits for them, and re-layouts  3.22 us (1%)
    psum x1, waiting for transfers between devices, shards(): lax.psum((part_gate_up.astype(jnp.bfloat16), part_act.astype(jnp.bfloat16...  146 us
    all_to_all x1, blocking collectives, shards(): lax.all_to_all(send, 'expert', split_axis=0, concat_axis=0, tiled=True)  61.8 us
    all_to_all x1, waiting for transfers between devices, shards(): lax.all_to_all(slot_grad.reshape(experts, MOST, slab_width).astype(jnp.bf...  18.5 us
    all_to_all x1, starting transfers between devices, shards(): lax.all_to_all(slot_grad.reshape(experts, MOST, slab_width).astype(jnp.bf...  10 us
  transfers between devices with their start and end apart: 2, of which 2 were waited for; matrix products, arithmetic and copies ran while one was open for 4% of the time, Pallas kernels for 0%

profile of v6, /device:TPU:32, one launch (start us, length us, event | category | flops | bytes accessed | tf_op | source)
XLA Modules:
  0.0 287.7 jit_solution(8520846011147565709)
XLA Ops:
  7.2 0.0 copy-start
  7.2 0.0 all-reduce.3.cloned.1.call-start
  7.2 0.8 copy.14
  8.0 0.7 copy.13
  8.7 0.7 eq.40
  9.4 1.2 reduce-window.6
  10.5 0.2 slice_reduce_fusion
  10.8 0.1 fusion.27
  10.9 1.2 multiply_convert_fusion.4
  12.1 2.3 fusion.11
  14.4 61.8 %all_to_all.10 = bf16[32,32,1024]{2,1,0:T(8,128)(2,1)S(1)} all-to-all(bf16[32,32,1024]{2,1,0:T(8,128)(2,1)S(1)} %bitcast.48), channel_id=1, replica_groups=mesh['dp'=8,'expert'=32] {'expert'}, dimensions={0} | all-to-all | bytes 4194304 | tf_op jit(solution)/shard_map/all_to_all | solution.py:48
  76.2 0.2 fusion.33
  76.4 0.0 copy-start.8
  76.4 0.0 copy-start.9
  76.4 2.6 convolution_convert_fusion.1
  79.0 0.0 copy-done.6
  79.0 0.0 copy-done.9
  79.0 4.3 %convolution_convert_fusion = bf16[1024,2048]{1,0:T(8,128)(2,1)} fusion(bf16[1024,512]{1,0:T(8,128)(2,1)S(1)} %bitcast.45, bf16[512,1024]{1,0:T(8,128)(2,1)S(1)} %bitcast.59, bf16[512,1024]{1,0:T(8,128)(2,1)S(1)} %bitcast.61), kind=kOutput, calls=%fused_computation.12 | convolution fusion | flops 2153775104 | bytes 7340032 | tf_op jit(solution)/shard_map/dot_general | solution.py:58
  83.4 0.0 all-reduce.3.cloned.1.call-update
  83.4 146.2 %all-reduce.3.cloned.1.call-done = (bf16[1024,1024]{1,0:T(8,128)(2,1)}, bf16[1024,2048]{1,0:T(8,128)(2,1)}) async-done(((bf16[1024,1024]{1,0:T(8,128)(2,1)}, bf16[1024,2048]{1,0:T(8,128)(2,1)}), (bf16[1024,1024]{1,0:T(8,128)(2,1)}, bf16[1024,2048]{1,0:T(8,128)(2,1)})) %all-reduce.3.cloned.1.call-update) | async-done | bytes 6291472 | tf_op jit(solution)/shard_map/psum | solution.py:62
  229.6 3.4 %convert_element_type.52 = f32[1024,2048]{1,0:T(8,128)S(1)} convert(bf16[1024,2048]{1,0:T(8,128)(2,1)} %get-tuple-element.9) | non-fusion elementwise | flops 2097152 | bytes 12582912 | tf_op jit(solution)/shard_map/convert_element_type | solution.py:65
  233.0 0.0 copy-start.10
  233.1 2.6 fusion.2
  235.7 0.6 copy-done.1
  236.3 3.4 %fusion.13 = bf16[1024,512]{1,0:T(8,128)(2,1)} fusion(bf16[1024,1024]{1,0:T(8,128)(2,1)S(1)} %get-tuple-element.7, bf16[1024,1024]{1,0:T(8,128)(2,1)S(1)} %get-tuple-element.6, bf16[512,1024]{1,0:T(8,128)(2,1)S(1)} %bitcast.60, bf16[512,1024]{1,0:T(8,128)(2,1)S(1)} %bitcast.62), kind=kOutput, calls=%fused_computation.23 | convolution fusion | flops 2160590848 | bytes 7340032 | tf_op jit(solution)/shard_map/dot_general | solution.py:71
  239.6 10.0 %all-to-all-start.1 = ((bf16[32,32,512]{2,1,0:T(8,128)(2,1)}), bf16[32,32,512]{2,1,0:T(8,128)(2,1)S(1)}, u32[]{:S(2)}, u32[]{:S(2)}) async-start(bf16[32,32,512]{2,1,0:T(8,128)(2,1)} %bitcast.50), calls=%async_computation.1 | async-start | bytes 2097152 | tf_op jit(solution)/shard_map/all_to_all | solution.py:86
  249.7 4.3 %convolution_bitcast_fusion.1 = f32[1,512,1024]{2,1,0:T(8,128)} fusion(bf16[1024,512]{1,0:T(8,128)(2,1)S(1)} %bitcast.46, bf16[1024,1024]{1,0:T(8,128)(2,1)} %copy-done.4), kind=kOutput, calls=%fused_computation.22 | convolution fusion | flops 1073741824 | bytes 5242880 | tf_op jit(solution)/shard_map/dot_general | solution.py:77
  254.0 4.2 %convolution_bitcast_fusion = f32[1,512,1024]{2,1,0:T(8,128)} fusion(bf16[1024,512]{1,0:T(8,128)(2,1)S(1)} %bitcast.47, bf16[1024,1024]{1,0:T(8,128)(2,1)} %copy-done.3), kind=kOutput, calls=%fused_computation.21 | convolution fusion | flops 1073741824 | bytes 5242880 | tf_op jit(solution)/shard_map/dot_general | solution.py:80
  258.2 2.7 fusion.12
  260.9 18.5 %all-to-all-done.1 = bf16[32,32,512]{2,1,0:T(8,128)(2,1)S(1)} async-done(((bf16[32,32,512]{2,1,0:T(8,128)(2,1)}), bf16[32,32,512]{2,1,0:T(8,128)(2,1)S(1)}, u32[]{:S(2)}, u32[]{:S(2)}) %all-to-all-start.1) | async-done | bytes 1048608 | tf_op jit(solution)/shard_map/all_to_all | solution.py:86
  279.4 0.8 fusion.9
  280.1 0.8 fusion.24
  (19 shorter events, 0.1 us)
Async XLA Ops:
  7.2 69.2 %copy-start = (bf16[1,1024,512]{2,1,0:T(8,128)(2,1)S(1)}, bf16[1,1024,512]{2,1,0:T(8,128)(2,1)}, u32[]{:S(2)}) copy-start(bf16[1,1024,512]{2,1,0:T(8,128)(2,1)} %param.13) | copy-start | bytes 3145732
  7.2 222.4 %all-reduce.3.cloned.1.call-start = ((), (), s32[]{:S(2)}) async-start(), calls=%async_computation.2 | async-start | bytes 12582912 | tf_op jit(solution)/shard_map/psum | solution.py:62
  76.4 2.7 copy-start.6
  76.4 2.6 copy-start.8
  76.4 2.6 copy-start.9
  229.6 3.4 %copy-start.5 = (bf16[1024,1024]{1,0:T(8,128)(2,1)S(1)}, bf16[1024,1024]{1,0:T(8,128)(2,1)}, u32[]{:S(2)}) copy-start(bf16[1024,1024]{1,0:T(8,128)(2,1)} %get-tuple-element.8) | copy-start | bytes 6291460
  233.0 3.2 %copy-start.1 = (f32[1024,2048]{1,0:T(8,128)}, f32[1024,2048]{1,0:T(8,128)S(1)}, u32[]{:S(2)}) copy-start(f32[1024,2048]{1,0:T(8,128)S(1)} %convert_element_type.52) | copy-start | bytes 25165828
  233.0 3.2 %copy-start.10 = (bf16[1,512,1024]{2,1,0:T(8,128)(2,1)S(1)}, bf16[1,512,1024]{2,1,0:T(8,128)(2,1)}, u32[]{:S(2)}) copy-start(bf16[1,512,1024]{2,1,0:T(8,128)(2,1)} %param.11) | copy-start | bytes 3145732
  236.3 3.4 %copy-start.3 = (bf16[1024,1024]{1,0:T(8,128)(2,1)}, bf16[1024,1024]{1,0:T(8,128)(2,1)S(1)}, u32[]{:S(2)}) copy-start(bf16[1024,1024]{1,0:T(8,128)(2,1)S(1)} %get-tuple-element.7) | copy-start | bytes 6291460
  236.3 3.4 %copy-start.4 = (bf16[1024,1024]{1,0:T(8,128)(2,1)}, bf16[1024,1024]{1,0:T(8,128)(2,1)S(1)}, u32[]{:S(2)}) copy-start(bf16[1024,1024]{1,0:T(8,128)(2,1)S(1)} %get-tuple-element.6) | copy-start | bytes 6291460
  239.6 39.7 %all-to-all-start.1 = ((bf16[32,32,512]{2,1,0:T(8,128)(2,1)}), bf16[32,32,512]{2,1,0:T(8,128)(2,1)S(1)}, u32[]{:S(2)}, u32[]{:S(2)}) async-start(bf16[32,32,512]{2,1,0:T(8,128)(2,1)} %bitcast.50), calls=%async_computation.1 | async-start | bytes 2097152 | tf_op jit(solution)/shard_map/all_to_all | solution.py:86
  249.7 8.5 %copy-start.2 = (f32[1024,2048]{1,0:T(8,128)S(1)}, f32[1024,2048]{1,0:T(8,128)}, u32[]{:S(2)}) copy-start(f32[1024,2048]{1,0:T(8,128)} %copy-done.1) | copy-start | bytes 25165828
  249.7 8.5 %copy-start.7 = (bf16[32,32,512]{2,1,0:T(8,128)(2,1)S(1)}, bf16[32,32,512]{2,1,0:T(8,128)(2,1)}, u32[]{:S(2)}) copy-start(bf16[32,32,512]{2,1,0:T(8,128)(2,1)} %copy-done.6) | copy-start | bytes 3145732
Sparse Core Ops, SparseCore 0:
  83.5 146.0 all-reduce.2

commit v7 on v3

--- a/solution.py
+++ b/solution.py
@@ -28,8 +28,12 @@
     owners = lax.axis_size("expert")
     experts = owners * w_gate.shape[0]
     pick_ids = expert_ids.T.reshape(-1)
-    onehot = (pick_ids[:, None] == jnp.arange(experts, dtype=jnp.int32)[None, :]).astype(jnp.int32)
-    rank_in = jnp.sum((jnp.cumsum(onehot, axis=0) - 1) * onehot, axis=1)
+    onehot = (pick_ids[:, None] == jnp.arange(experts, dtype=jnp.int32)[None, :]).astype(jnp.bfloat16)
+    picks = pick_ids.shape[0]
+    order = jnp.arange(picks, dtype=jnp.int32)
+    earlier = (order[None, :] < order[:, None]).astype(jnp.bfloat16)
+    before = jnp.dot(earlier, onehot, preferred_element_type=jnp.float32)
+    rank_in = jnp.sum(before * onehot.astype(jnp.float32), axis=1).astype(jnp.int32)
     slot_of = pick_ids * MOST + rank_in
     placing = (jnp.arange(experts * MOST, dtype=jnp.int32)[:, None] == slot_of[None, :]).astype(
         jnp.bfloat16

time: 287 us -> 285 us (level)
  no operation moved by 1% of the time
where the time goes in v7:
time: 285 us
  waiting for transfers between devices  166 us (58%)
  blocking collectives  61.8 us (22%)
  matrix products  24.4 us (9%)
  between operations  14.2 us (5%)
  starting transfers between devices  10.1 us (4%)
  other arithmetic  6.21 us (2%)
  local copies, waits for them, and re-layouts  2.97 us (1%)
    psum x1, waiting for transfers between devices, shards(): lax.psum(part_up.astype(jnp.bfloat16), 'dp').astype(jnp.float32)  146 us
    all_to_all x1, blocking collectives, shards(): lax.all_to_all(send, 'expert', split_axis=0, concat_axis=0, tiled=True)  61.8 us
    all_to_all x1, waiting for transfers between devices, shards(): lax.all_to_all(slot_grad.reshape(experts, MOST, slab_width).astype(jnp.bf...  19.3 us
    all_to_all x1, starting transfers between devices, shards(): lax.all_to_all(slot_grad.reshape(experts, MOST, slab_width).astype(jnp.bf...  10 us
  transfers between devices with their start and end apart: 2, of which 2 were waited for; matrix products, arithmetic and copies ran while one was open for 3% of the time, Pallas kernels for 0%

profile of v7, /device:TPU:32, one launch (start us, length us, event | category | flops | bytes accessed | tf_op | source)
XLA Modules:
  0.0 285.1 jit_solution(2284455037294095577)
XLA Ops:
  7.2 0.0 copy-start
  7.2 0.0 all-reduce.3.cloned.1.call-start
  7.2 0.8 copy.11
  8.0 0.3 fusion.17
  8.3 0.7 copy.12
  9.0 1.2 multiply_convert_fusion
  10.2 2.3 fusion.13
  12.5 61.8 %all_to_all.10 = bf16[32,32,1024]{2,1,0:T(8,128)(2,1)S(1)} all-to-all(bf16[32,32,1024]{2,1,0:T(8,128)(2,1)S(1)} %bitcast.45), channel_id=1, replica_groups=mesh['dp'=8,'expert'=32] {'expert'}, dimensions={0} | all-to-all | bytes 4194304 | tf_op jit(solution)/shard_map/all_to_all | solution.py:52
  74.2 0.2 fusion.36
  74.4 0.0 copy-start.6
  74.5 0.0 copy-start.9
  74.5 2.6 convolution_convert_fusion
  77.1 2.6 convolution_convert_fusion.1
  79.6 2.6 convolution_convert_fusion.2
  82.2 0.0 all-reduce.3.cloned.1.call-update
  82.3 146.2 %all-reduce.3.cloned.1.call-done = (bf16[1024,1024]{1,0:T(8,128)(2,1)}, bf16[1024,1024]{1,0:T(8,128)(2,1)}, bf16[1024,1024]{1,0:T(8,128)(2,1)}) async-done(((bf16[1024,1024]{1,0:T(8,128)(2,1)}, bf16[1024,1024]{1,0:T(8,128)(2,1)}, bf16[1024,1024]{1,0:T(8,128)(2,1)}), (bf16[1024,1024]{1,0:T(8,128)(2,1)}, bf16[1024,1024]{1,0:T(8,128)(2,1)}, bf16[1024,1024]{1,0:T(8,128)(2,1)})) %all-reduce.3.cloned.1.call-update) | async-done | bytes 6291472 | tf_op jit(solution)/shard_map/psum | solution.py:67
  228.5 4.2 %fusion = (bf16[1024,1024]{1,0:T(8,128)(2,1)S(1)}, bf16[1024,1024]{1,0:T(8,128)(2,1)S(1)}) fusion(bf16[1024,1024]{1,0:T(8,128)(2,1)} %get-tuple-element.9, bf16[1024,1024]{1,0:T(8,128)(2,1)} %get-tuple-element.10, bf16[1024,1024]{1,0:T(8,128)(2,1)} %get-tuple-element.8), kind=kLoop, calls=%fused_computation.6 | loop fusion | flops 16777216 | bytes 10485760 | tf_op jit(solution)/shard_map/convert_element_type | solution.py:22
  232.8 0.0 copy-start.1
  232.8 0.0 copy-start.3
  232.8 1.3 fusion.23
  234.1 0.0 copy-done.1
  234.1 0.7 copy-done.3
  234.8 2.2 add_convert_fusion
  237.0 10.0 %all-to-all-start.1 = ((bf16[32,32,512]{2,1,0:T(8,128)(2,1)}), bf16[32,32,512]{2,1,0:T(8,128)(2,1)S(1)}, u32[]{:S(2)}, u32[]{:S(2)}) async-start(bf16[32,32,512]{2,1,0:T(8,128)(2,1)} %bitcast.47), calls=%async_computation.1 | async-start | bytes 2097152 | tf_op jit(solution)/shard_map/all_to_all | solution.py:87
  247.1 0.0 copy-start.2
  247.1 4.3 %convolution_bitcast_fusion.1 = f32[1,512,1024]{2,1,0:T(8,128)} fusion(bf16[1024,512]{1,0:T(8,128)(2,1)S(1)} %bitcast.43, bf16[1024,1024]{1,0:T(8,128)(2,1)} %copy-done.3), kind=kOutput, calls=%fused_computation.26 | convolution fusion | flops 1073741824 | bytes 5242880 | tf_op jit(solution)/shard_map/dot_general | solution.py:78
  251.4 2.6 convolution_bitcast_fusion
  254.0 0.6 copy-done.7
  254.6 2.8 fusion.14
  257.4 19.3 %all-to-all-done.1 = bf16[32,32,512]{2,1,0:T(8,128)(2,1)S(1)} async-done(((bf16[32,32,512]{2,1,0:T(8,128)(2,1)}), bf16[32,32,512]{2,1,0:T(8,128)(2,1)S(1)}, u32[]{:S(2)}, u32[]{:S(2)}) %all-to-all-start.1) | async-done | bytes 1048608 | tf_op jit(solution)/shard_map/all_to_all | solution.py:87
  276.7 0.8 fusion.11
  277.5 0.8 fusion.31
  (12 shorter events, 0.0 us)
Async XLA Ops:
  7.2 67.3 %copy-start = (bf16[1,512,1024]{2,1,0:T(8,128)(2,1)S(1)}, bf16[1,512,1024]{2,1,0:T(8,128)(2,1)}, u32[]{:S(2)}) copy-start(bf16[1,512,1024]{2,1,0:T(8,128)(2,1)} %param.11) | copy-start | bytes 3145732
  7.2 221.3 %all-reduce.3.cloned.1.call-start = ((), (), s32[]{:S(2)}) async-start(), calls=%async_computation.2 | async-start | bytes 12582912 | tf_op jit(solution)/shard_map/psum | solution.py:67
  74.4 5.2 %copy-start.6 = (bf16[32,32,512]{2,1,0:T(8,128)(2,1)}, bf16[32,32,512]{2,1,0:T(8,128)(2,1)S(1)}, u32[]{:S(2)}) copy-start(bf16[32,32,512]{2,1,0:T(8,128)(2,1)S(1)} %get-tuple-element.13) | copy-start | bytes 3145732
  74.5 2.6 copy-start.9
  77.1 2.6 copy-start.8
  232.8 1.3 copy-start.1
  232.8 2.0 copy-start.3
  237.0 39.7 %all-to-all-start.1 = ((bf16[32,32,512]{2,1,0:T(8,128)(2,1)}), bf16[32,32,512]{2,1,0:T(8,128)(2,1)S(1)}, u32[]{:S(2)}, u32[]{:S(2)}) async-start(bf16[32,32,512]{2,1,0:T(8,128)(2,1)} %bitcast.47), calls=%async_computation.1 | async-start | bytes 2097152 | tf_op jit(solution)/shard_map/all_to_all | solution.py:87
  247.1 4.3 %copy-start.2 = (bf16[1024,1024]{1,0:T(8,128)(2,1)S(1)}, bf16[1024,1024]{1,0:T(8,128)(2,1)}, u32[]{:S(2)}) copy-start(bf16[1024,1024]{1,0:T(8,128)(2,1)} %copy-done.1) | copy-start | bytes 6291460
  251.4 2.6 copy-start.4
  251.4 2.6 copy-start.5
  251.4 3.2 %copy-start.7 = (bf16[32,32,512]{2,1,0:T(8,128)(2,1)S(1)}, bf16[32,32,512]{2,1,0:T(8,128)(2,1)}, u32[]{:S(2)}) copy-start(bf16[32,32,512]{2,1,0:T(8,128)(2,1)} %copy-done.6) | copy-start | bytes 3145732
Sparse Core Ops, SparseCore 0:
  82.4 146.0 all-reduce.2
